TPU v7x, 256 devices: a whole 4x4x8 slice. The times are simulated.
256 devices in a mesh: seq: 32 (over z, y_lo, core), tp: 8 (over y_hi, x).
Axes of the slice: x: 4, y: 4 (y_hi: 2, y_lo: 2; y = y_hi * 2 + y_lo), z: 8, core: 2. Of those that a mesh axis runs over, the one named last changes fastest.
Arguments:
- qkv_se: bfloat16 [16384, 3, 4096], P('seq', None, 'tp'), may hold values from -6 to 6
- residual: bfloat16 [16384, 4096], P('seq', 'tp'), may hold values from -108 to 108
- taps_se: bfloat16 [256, 7], P('tp'), may hold values from -2 to 2
- skip_se: bfloat16 [4096], P('tp'), may hold values from 0.5 to 1.5
- w_out: bfloat16 [4096, 4096], P('tp', 'seq'), may hold values from -0.1875 to 0.1875
- norm_gain: bfloat16 [4096], replicated, may hold values from 0.5 to 1.5
- w_in: bfloat16 [4096, 3, 4096], P('seq', None, 'tp'), may hold values from -0.09375 to 0.09375
- taps_mr: bfloat16 [256, 128], P('tp'), may hold values from -0.5 to 0.5
- skip_mr: bfloat16 [4096], P('tp'), may hold values from 0.5 to 1.5
Outputs:
- mixed: bfloat16 [16384, 4096], P('seq', 'tp')
All inputs are finite; a program needn't handle non-finite values.
Results may differ from a plain program's by a relative error of at most 0.0085.
Values may be sent and summed in bfloat16 or wider, within the bound.
No kernel may reach another device: no remote copies, remote signals or barrier semaphores. Data moves between devices by JAX's collectives and lax.ppermute only.
A program may use at most 64 MiB of HBM per device.

v0:
```python
import jax
import jax.numpy as jnp
from jax import lax
from jax.sharding import PartitionSpec as P

GROUP = 16
SE_TAPS = 7
MR_TAPS = 128


norm_eps = 1e-05


def shifted(block, axis, distance):
    devices = range(lax.axis_size(axis))
    route = [(i - distance, i) for i in devices if i - distance in devices]
    return lax.ppermute(block, axis, route)


def seq_coords(index):
    return index // 4, (index // 2) % 2, index % 2


def seq_of(z, y_lo, core):
    return z * 4 + y_lo * 2 + core


def exchange(block, axis, pairs):
    return lax.ppermute(block, axis, pairs)


def gather_rows(piece):
    seq_size = lax.axis_size("seq")
    z_size = seq_size // 4
    me = lax.axis_index("seq")
    other = exchange(piece, "seq", [(i, i ^ 2) for i in range(seq_size)])
    mine_first = (me // 2) % 2 == 0
    block = jnp.stack(
        [jnp.where(mine_first, piece, other), jnp.where(mine_first, other, piece)]
    )
    ahead = []
    behind = []
    for i in range(seq_size):
        z, y_lo, core = seq_coords(i)
        ahead.append((i, seq_of((z + 1) % z_size, y_lo, core)))
        behind.append((i, seq_of((z - 1) % z_size, y_lo, core)))
    core_pair = [(i, i ^ 1) for i in range(seq_size)]
    blocks = [(0, block)]
    moving_up = block
    moving_down = block
    for step in range(1, z_size // 2 + 1):
        moving_up = exchange(moving_up, "seq", ahead)
        blocks.append((step, moving_up))
        if step < z_size // 2:
            moving_down = exchange(moving_down, "seq", behind)
            blocks.append((z_size - step, moving_down))
    return [(k, mine, exchange(mine, "seq", core_pair)) for k, mine in blocks]


def ring_rows(pieces):
    return jnp.stack([jnp.stack([mine, partner]) for _, mine, partner in sorted(pieces)])


def ring_features(gathered, rows):
    z_size = gathered.shape[0]
    me = lax.axis_index("seq")
    my_z = me // 4
    my_core = me % 2
    features = gathered.reshape(z_size, gathered.shape[1], 2, 2, rows)
    reverse = features[::-1]
    doubled = jnp.concatenate([reverse, reverse], axis=0)
    start = (z_size - 1 - my_z) % z_size
    by_offset = lax.dynamic_slice_in_dim(doubled, start, z_size, axis=0)
    return jnp.where(my_core == 0, by_offset, by_offset[:, :, :, ::-1])


def tp_sum(value):
    tp_size = lax.axis_size("tp")
    total = value
    bit = 1
    while bit < tp_size:
        total = total + lax.ppermute(total, "tp", [(i, i ^ bit) for i in range(tp_size)])
        bit *= 2
    return total


def toeplitz_pair(taps):
    offsets = lax.broadcasted_iota(jnp.int32, (MR_TAPS, MR_TAPS), 0) - lax.broadcasted_iota(
        jnp.int32, (MR_TAPS, MR_TAPS), 1
    )
    lag_ids = lax.broadcasted_iota(jnp.int32, (MR_TAPS, MR_TAPS, MR_TAPS), 0)
    picks = (jnp.remainder(offsets, MR_TAPS)[None] == lag_ids).astype(jnp.bfloat16)
    table = jnp.einsum("gj,jts->gts", taps, picks, preferred_element_type=jnp.float32).astype(
        jnp.bfloat16
    )
    lower = jnp.where(offsets[None] >= 0, table, jnp.zeros_like(table))
    upper = jnp.where(offsets[None] < 0, table, jnp.zeros_like(table))
    return (lower, upper)


def project_out(y_se, w_out):
    tp_size = lax.axis_size("tp")
    stacked = lax.all_gather(w_out, "seq", axis=0, tiled=False)
    per_tp = stacked.reshape(tp_size, stacked.shape[0] // tp_size, *stacked.shape[1:])
    partial = jnp.einsum("tc,kjcf->ktjf", y_se, per_tp, preferred_element_type=jnp.float32)
    return partial.reshape(tp_size, y_se.shape[0], -1)


def per_device(qkv_se, residual, taps_se, skip_se, w_out, norm_gain, w_in, taps_mr, skip_mr):
    row_count = qkv_se.shape[0]
    chan_width = qkv_se.shape[2]
    local_groups = chan_width // GROUP
    query_se = qkv_se[:, 0].astype(jnp.float32)
    u_se = (qkv_se[:, 1].astype(jnp.float32) * qkv_se[:, 2].astype(jnp.float32)).astype(
        jnp.bfloat16
    )
    incoming_se = shifted(u_se[row_count - (SE_TAPS - 1) :], "seq", 1)
    extended = jnp.concatenate([incoming_se, u_se], axis=0).astype(jnp.float32)
    per_channel = jnp.repeat(taps_se.astype(jnp.float32), GROUP, axis=0)
    conv_se = jnp.zeros((row_count, chan_width), jnp.float32)
    for tap_index in range(SE_TAPS):
        begin = SE_TAPS - 1 - tap_index
        conv_se = conv_se + per_channel[:, tap_index] * extended[begin : begin + row_count]
    y_se = (query_se * (conv_se + skip_se.astype(jnp.float32) * u_se.astype(jnp.float32))).astype(
        jnp.bfloat16
    )
    gain_full = norm_gain.astype(jnp.float32)
    partial_out = project_out(y_se, w_out)
    share = lax.psum_scatter(partial_out, "tp", scatter_dimension=0, tiled=True)[0]
    w_full = ring_rows(gather_rows(w_in))
    share, w_full = lax.optimization_barrier((share, w_full))
    stream = residual.astype(jnp.float32) + share
    squares = tp_sum(jnp.sum(stream * stream, axis=1))
    scale = lax.rsqrt(squares / (chan_width * lax.axis_size("tp")) + norm_eps)
    my_gain = lax.dynamic_slice_in_dim(gain_full, lax.axis_index("tp") * chan_width, chan_width, 0)
    normed = (stream * scale[:, None] * my_gain).astype(jnp.bfloat16)
    gathered = lax.all_gather(normed, "tp", axis=0, tiled=False)
    proj = jnp.einsum(
        "ktycr,kcyrin->tin",
        ring_features(gathered, w_in.shape[0]),
        w_full,
        preferred_element_type=jnp.float32,
    )
    query_mr = proj[:, 0]
    u_mr = (proj[:, 1] * proj[:, 2]).astype(jnp.bfloat16)
    lower, upper = toeplitz_pair(taps_mr)
    block_count = row_count // MR_TAPS
    blocks = u_mr.reshape(block_count, MR_TAPS, local_groups, GROUP)
    inside = jnp.einsum("gts,bsgc->btgc", lower, blocks, preferred_element_type=jnp.float32)
    tail_rows = shifted(blocks[block_count - 1], "seq", 1)
    earlier = jnp.concatenate([tail_rows[None], blocks[: block_count - 1]], axis=0)
    conv_mr = inside + jnp.einsum(
        "gts,bsgc->btgc", upper, earlier, preferred_element_type=jnp.float32
    )
    conv_mr = conv_mr.reshape(row_count, chan_width)
    return (query_mr * (conv_mr + skip_mr.astype(jnp.float32) * u_mr.astype(jnp.float32))).astype(
        jnp.bfloat16
    )


def solution(mesh):
    placed = (
        P("seq", None, "tp"),
        P("seq", "tp"),
        P("tp", None),
        P("tp"),
        P("tp", "seq"),
        P(),
        P("seq", None, "tp"),
        P("tp", None),
        P("tp"),
    )
    return jax.shard_map(
        per_device, mesh=mesh, in_specs=placed, out_specs=P("seq", "tp"), check_vma=False
    )
```

profile of v0, /device:TPU:105, one launch (start us, length us, event | category | flops | bytes accessed | tf_op | source)
XLA Modules:
  0.0 365.0 jit_solution(10622153072527193709)
XLA Ops:
  8.7 5.2 %collective-permute-start = (bf16[6,512]{1,0:T(8,128)(2,1)S(1)}, bf16[6,512]{1,0:T(8,128)(2,1)S(1)}, u32[]{:S(2)}, u32[]{:S(2)}) collective-permute-start(bf16[6,512]{1,0:T(8,128)(2,1)S(1)} %slice_bitcast_fusion.1), channel_id=1, source_target_pairs={{0,8},{8,16},{16,24},{24,32},{32,40},{40,48},{48,56},{56,64},{64,7... | collective-permute-start | bytes 18440 | tf_op jit(solution)/shard_map/ppermute | solution.py:17
  16.3 59.7 %all-gather.5.cloned.1.call-done = bf16[16384,128]{1,0:T(8,128)(2,1)} async-done(((bf16[512,128]{1,0:T(8,128)(2,1)}), bf16[16384,128]{1,0:T(8,128)(2,1)}) %all-gather.5.cloned.1.call-update) | async-done | bytes 4194320 | tf_op jit(solution)/shard_map/all_gather | solution.py:103
  76.0 8.5 %fusion.37 = f32[512,8,4,128]{0,3,2,1:T(8,128)} fusion(bf16[8,4,512,128]{3,2,1,0:T(8,128)(2,1)} %bitcast.160, f32[518,512]{1,0:T(8,128)S(1)} %maximum_convert_fusion, f32[512]{0:T(512)S(1)} %convert_element_type.78, f32[512]{0:T(512)S(1)} %bitcast.154, f32[512]{0:T(512)S(1)} %bitcast.155, f32[512]{0:T(512)S(1)} %bitcast.156, f32[512]{0:T(512)S(1)} %bitcast.157, ...), kind=kOutput, calls=%fused_computation.67 | convolution fusion | flops 2152464384 | bytes 20987904 | tf_op jit(solution)/shard_map/tc,kjcf->ktjf/dot_general | solution.py:105
  84.6 9.1 %copy.31 = f32[8,512,512]{2,1,0:T(8,128)} copy(f32[8,512,512]{1,2,0:T(8,128)} %bitcast.134) | data formatting | bytes 16777216 | tf_op jit(solution)/shard_map/reshape | solution.py:106
  95.9 9.1 %collective-permute-done.1 = bf16[128,3,512]{2,0,1:T(8,128)(2,1)S(1)} collective-permute-done((bf16[128,3,512]{2,0,1:T(8,128)(2,1)S(1)}, bf16[128,3,512]{2,0,1:T(8,128)(2,1)S(1)}, u32[]{:S(2)}, u32[]{:S(2)}) %collective-permute-start.1) | collective-permute-done | bytes 393248 | tf_op jit(solution)/shard_map/ppermute | solution.py:29
  105.3 2.6 collective-permute-start.3
  107.9 15.8 %collective-permute-done.3 = bf16[2,128,3,512]{3,1,2,0:T(8,128)(2,1)S(1)} collective-permute-done((bf16[2,128,3,512]{3,1,2,0:T(8,128)(2,1)S(1)}, bf16[2,128,3,512]{3,1,2,0:T(8,128)(2,1)S(1)}, u32[]{:S(2)}, u32[]{:S(2)}) %collective-permute-start.3) | collective-permute-done | bytes 786464 | tf_op jit(solution)/shard_map/ppermute | solution.py:29
  123.6 3.4 collective-permute-start.5
  127.1 14.9 %collective-permute-done.5 = bf16[2,128,3,512]{3,1,2,0:T(8,128)(2,1)S(1)} collective-permute-done((bf16[2,128,3,512]{3,1,2,0:T(8,128)(2,1)S(1)}, bf16[2,128,3,512]{3,1,2,0:T(8,128)(2,1)S(1)}, u32[]{:S(2)}, u32[]{:S(2)}) %collective-permute-start.5) | collective-permute-done | bytes 786464 | tf_op jit(solution)/shard_map/ppermute | solution.py:29
  142.0 3.4 collective-permute-start.7
  145.4 3.1 collective-permute-start.2
  148.5 10.9 %collective-permute-done.7 = bf16[2,128,3,512]{3,1,2,0:T(8,128)(2,1)S(1)} collective-permute-done((bf16[2,128,3,512]{3,1,2,0:T(8,128)(2,1)S(1)}, bf16[2,128,3,512]{3,1,2,0:T(8,128)(2,1)S(1)}, u32[]{:S(2)}, u32[]{:S(2)}) %collective-permute-start.7) | collective-permute-done | bytes 786464 | tf_op jit(solution)/shard_map/ppermute | solution.py:29
  159.4 3.4 collective-permute-start.9
  162.8 4.0 %collective-permute-start.4 = (bf16[2,128,3,512]{3,1,2,0:T(8,128)(2,1)S(1)}, bf16[2,128,3,512]{3,1,2,0:T(8,128)(2,1)S(1)}, u32[]{:S(2)}, u32[]{:S(2)}) collective-permute-start(bf16[2,128,3,512]{3,1,2,0:T(8,128)(2,1)S(1)} %collective-permute-done.3), channel_id=1, source_target_pairs={{0,8},{8,0},{16,24},{24,16},{32,40},{40,32},{48,56},{56,48},{64,72... | collective-permute-start | bytes 2359304 | tf_op jit(solution)/shard_map/ppermute | solution.py:29
  167.3 8.7 %collective-permute-done.9 = bf16[2,128,3,512]{3,1,2,0:T(8,128)(2,1)S(1)} collective-permute-done((bf16[2,128,3,512]{3,1,2,0:T(8,128)(2,1)S(1)}, bf16[2,128,3,512]{3,1,2,0:T(8,128)(2,1)S(1)}, u32[]{:S(2)}, u32[]{:S(2)}) %collective-permute-start.9) | collective-permute-done | bytes 786464 | tf_op jit(solution)/shard_map/ppermute | solution.py:29
  176.0 4.6 %collective-permute-start.10 = (bf16[2,128,3,512]{3,1,2,0:T(8,128)(2,1)S(1)}, bf16[2,128,3,512]{3,1,2,0:T(8,128)(2,1)S(1)}, u32[]{:S(2)}, u32[]{:S(2)}) collective-permute-start(bf16[2,128,3,512]{3,1,2,0:T(8,128)(2,1)S(1)} %collective-permute-done.9), channel_id=1, source_target_pairs={{0,8},{8,0},{16,24},{24,16},{32,40},{40,32},{48,56},{56,48},{64,72... | collective-permute-start | bytes 2359304 | tf_op jit(solution)/shard_map/ppermute | solution.py:29
  180.6 3.4 collective-permute-start.14
  194.8 18.7 %reduce-scatter.2.cloned.1.call-done = f32[1,512,512]{2,1,0:T(8,128)} async-done(((f32[8,512,512]{2,1,0:T(8,128)}), f32[1,512,512]{2,1,0:T(8,128)}) %reduce-scatter.2.cloned.1.call-update) | async-done | bytes 1048592 | tf_op jit(solution)/shard_map/reduce_scatter | solution.py:129
  215.0 2.4 collective-permute-done.17
  218.6 2.8 collective-permute-done.18
  225.3 2.2 multiply_convert_fusion
  227.7 3.3 select_bitcast_fusion
  231.0 74.7 %all-gather.7.cloned.1.call-done = bf16[4096,512]{1,0:T(8,128)(2,1)} async-done(((bf16[512,512]{1,0:T(8,128)(2,1)}), bf16[4096,512]{1,0:T(8,128)(2,1)}) %all-gather.7.cloned.1.call-update) | async-done | bytes 4194320 | tf_op jit(solution)/shard_map/all_gather | solution.py:137
  305.8 6.9 %reshape.82 = bf16[8,512,2,2,128]{4,3,2,1,0:T(2,128)(2,1)} reshape(bf16[4096,512]{1,0:T(8,128)(2,1)} %all-gather.7.cloned.1.call-done) | data formatting | bytes 8388608 | tf_op jit(solution)/shard_map/reshape | solution.py:69
  312.7 5.1 %copy.32 = bf16[8,512,2,2,128]{4,1,2,0,3:T(8,128)(2,1)} copy(bf16[8,512,2,2,128]{4,3,2,1,0:T(2,128)(2,1)} %reshape.82) | data formatting | bytes 8388608 | tf_op jit(solution)/shard_map/reshape | solution.py:69
  317.8 4.6 %rev.6 = bf16[8,512,2,2,128]{4,1,2,0,3:T(8,128)(2,1)} reverse(bf16[8,512,2,2,128]{4,1,2,0,3:T(8,128)(2,1)} %copy.32), dimensions={0} | reverse | bytes 8388608 | tf_op jit(solution)/shard_map/rev | solution.py:70
  322.4 3.1 fusion.4
  326.6 9.5 %fusion.6 = f32[512,3,512]{0,2,1:T(8,128)S(1)} fusion(bf16[8,512,2,2,128,1]{4,1,2,5,0,3:T(8,128)(2,1)S(1)} %fusion.3, bf16[8,2,2,128,3,512]{5,3,4,2,1,0:T(8,128)(2,1)} %fusion.16), kind=kOutput, calls=%fused_computation.10 | convolution fusion | flops 6442450944 | bytes 19922944 | tf_op jit(solution)/shard_map/ktycr,kcyrin->tin/dot_general | solution.py:138
  340.6 6.5 %collective-permute-start.20 = (bf16[128,32,16]{0,2,1:T(8,128)(2,1)}, bf16[128,32,16]{0,2,1:T(8,128)(2,1)}, u32[]{:S(2)}, u32[]{:S(2)}) collective-permute-start(bf16[128,32,16]{0,2,1:T(8,128)(2,1)} %bitcast.51), channel_id=1, source_target_pairs={{0,8},{8,16},{16,24},{24,32},{32,40},{40,48},{48,56},{56,64},{64,7... | collective-permute-start | bytes 393224 | tf_op jit(solution)/shard_map/ppermute | solution.py:17
  347.2 3.2 fusion.32
  352.4 2.5 fusion.18
  356.4 2.0 copy.39
  (79 shorter events, 34.0 us)
Async XLA Ops:
  6.5 221.1 %copy-start = (bf16[32,128]{1,0:T(8,128)(2,1)S(1)}, bf16[32,128]{1,0:T(8,128)(2,1)}, u32[]{:S(2)}) copy-start(bf16[32,128]{1,0:T(8,128)(2,1)} %param.16) | copy-start | bytes 24580
  6.5 9.6 %copy-start.4 = (bf16[512]{0:T(512)(128)(2,1)S(1)}, bf16[512]{0:T(512)(128)(2,1)}, u32[]{:S(2)}) copy-start(bf16[512]{0:T(512)(128)(2,1)} %param.12) | copy-start | bytes 3076
  6.5 69.5 %all-gather.5.cloned.1.call-start = ((), (), s32[]{:S(2)}) async-start(), calls=%async_computation.2 | async-start | bytes 4325376 | tf_op jit(solution)/shard_map/all_gather | solution.py:103
  7.3 206.2 %reduce-scatter.2.cloned.1.call-start = ((), (), s32[]{:S(2)}) async-start(), calls=%async_computation.1 | async-start | bytes 9437184 | tf_op jit(solution)/shard_map/reduce_scatter | solution.py:129
  8.7 7.5 %collective-permute-start = (bf16[6,512]{1,0:T(8,128)(2,1)S(1)}, bf16[6,512]{1,0:T(8,128)(2,1)S(1)}, u32[]{:S(2)}, u32[]{:S(2)}) collective-permute-start(bf16[6,512]{1,0:T(8,128)(2,1)S(1)} %slice_bitcast_fusion.1), channel_id=1, source_target_pairs={{0,8},{8,16},{16,24},{24,32},{32,40},{40,48},{48,56},{56,64},{64,7... | collective-permute-start | bytes 18440 | tf_op jit(solution)/shard_map/ppermute | solution.py:17
  93.7 1.0 copy-start.3
  93.7 212.0 %all-gather.7.cloned.1.call-start = ((), (), s32[]{:S(2)}) async-start(), calls=%async_computation.3 | async-start | bytes 4718592 | tf_op jit(solution)/shard_map/all_gather | solution.py:137
  94.7 10.4 %collective-permute-start.1 = (bf16[128,3,512]{2,0,1:T(8,128)(2,1)S(1)}, bf16[128,3,512]{2,0,1:T(8,128)(2,1)S(1)}, u32[]{:S(2)}, u32[]{:S(2)}) collective-permute-start(bf16[128,3,512]{2,0,1:T(8,128)(2,1)S(1)} %copy-done.3), channel_id=1, source_target_pairs={{0,16},{8,24},{16,0},{24,8},{32,48},{40,56},{48,32},{56,40},{64,80... | collective-permute-start | bytes 1179656 | tf_op jit(solution)/shard_map/ppermute | solution.py:29
  105.3 18.4 %collective-permute-start.3 = (bf16[2,128,3,512]{3,1,2,0:T(8,128)(2,1)S(1)}, bf16[2,128,3,512]{3,1,2,0:T(8,128)(2,1)S(1)}, u32[]{:S(2)}, u32[]{:S(2)}) collective-permute-start(bf16[2,128,3,512]{3,1,2,0:T(8,128)(2,1)S(1)} %get-tuple-element.12), channel_id=1, source_target_pairs={{0,32},{8,40},{16,48},{24,56},{32,64},{40,72},{48,80},{56,88},{64,... | collective-permute-start | bytes 2359304 | tf_op jit(solution)/shard_map/ppermute | solution.py:29
  123.6 18.3 %collective-permute-start.5 = (bf16[2,128,3,512]{3,1,2,0:T(8,128)(2,1)S(1)}, bf16[2,128,3,512]{3,1,2,0:T(8,128)(2,1)S(1)}, u32[]{:S(2)}, u32[]{:S(2)}) collective-permute-start(bf16[2,128,3,512]{3,1,2,0:T(8,128)(2,1)S(1)} %collective-permute-done.3), channel_id=1, source_target_pairs={{0,32},{8,40},{16,48},{24,56},{32,64},{40,72},{48,80},{56,88},{64,... | collective-permute-start | bytes 2359304 | tf_op jit(solution)/shard_map/ppermute | solution.py:29
  127.1 18.3 %collective-permute-start.11 = (bf16[2,128,3,512]{3,1,2,0:T(8,128)(2,1)S(1)}, bf16[2,128,3,512]{3,1,2,0:T(8,128)(2,1)S(1)}, u32[]{:S(2)}, u32[]{:S(2)}) collective-permute-start(bf16[2,128,3,512]{3,1,2,0:T(8,128)(2,1)S(1)} %get-tuple-element.12), channel_id=1, source_target_pairs={{0,224},{8,232},{16,240},{24,248},{32,0},{40,8},{48,16},{56,24},{6... | collective-permute-start | bytes 2359304 | tf_op jit(solution)/shard_map/ppermute | solution.py:29
  142.0 17.5 %collective-permute-start.7 = (bf16[2,128,3,512]{3,1,2,0:T(8,128)(2,1)S(1)}, bf16[2,128,3,512]{3,1,2,0:T(8,128)(2,1)S(1)}, u32[]{:S(2)}, u32[]{:S(2)}) collective-permute-start(bf16[2,128,3,512]{3,1,2,0:T(8,128)(2,1)S(1)} %collective-permute-done.5), channel_id=1, source_target_pairs={{0,32},{8,40},{16,48},{24,56},{32,64},{40,72},{48,80},{56,88},{64,... | collective-permute-start | bytes 2359304 | tf_op jit(solution)/shard_map/ppermute | solution.py:29
  145.4 17.5 %collective-permute-start.12 = (bf16[2,128,3,512]{3,1,2,0:T(8,128)(2,1)S(1)}, bf16[2,128,3,512]{3,1,2,0:T(8,128)(2,1)S(1)}, u32[]{:S(2)}, u32[]{:S(2)}) collective-permute-start(bf16[2,128,3,512]{3,1,2,0:T(8,128)(2,1)S(1)} %collective-permute-done.11), channel_id=1, source_target_pairs={{0,224},{8,232},{16,240},{24,248},{32,0},{40,8},{48,16},{56,24},{6... | collective-permute-start | bytes 2359304 | tf_op jit(solution)/shard_map/ppermute | solution.py:29
  145.4 21.5 %collective-permute-start.2 = (bf16[2,128,3,512]{3,1,2,0:T(8,128)(2,1)S(1)}, bf16[2,128,3,512]{3,1,2,0:T(8,128)(2,1)S(1)}, u32[]{:S(2)}, u32[]{:S(2)}) collective-permute-start(bf16[2,128,3,512]{3,1,2,0:T(8,128)(2,1)S(1)} %get-tuple-element.12), channel_id=1, source_target_pairs={{0,8},{8,0},{16,24},{24,16},{32,40},{40,32},{48,56},{56,48},{64,72... | collective-permute-start | bytes 2359304 | tf_op jit(solution)/shard_map/ppermute | solution.py:29
  159.4 16.6 %collective-permute-start.9 = (bf16[2,128,3,512]{3,1,2,0:T(8,128)(2,1)S(1)}, bf16[2,128,3,512]{3,1,2,0:T(8,128)(2,1)S(1)}, u32[]{:S(2)}, u32[]{:S(2)}) collective-permute-start(bf16[2,128,3,512]{3,1,2,0:T(8,128)(2,1)S(1)} %collective-permute-done.7), channel_id=1, source_target_pairs={{0,32},{8,40},{16,48},{24,56},{32,64},{40,72},{48,80},{56,88},{64,... | collective-permute-start | bytes 2359304 | tf_op jit(solution)/shard_map/ppermute | solution.py:29
  162.8 17.8 %collective-permute-start.13 = (bf16[2,128,3,512]{3,1,2,0:T(8,128)(2,1)S(1)}, bf16[2,128,3,512]{3,1,2,0:T(8,128)(2,1)S(1)}, u32[]{:S(2)}, u32[]{:S(2)}) collective-permute-start(bf16[2,128,3,512]{3,1,2,0:T(8,128)(2,1)S(1)} %collective-permute-done.12), channel_id=1, source_target_pairs={{0,224},{8,232},{16,240},{24,248},{32,0},{40,8},{48,16},{56,24},{6... | collective-permute-start | bytes 2359304 | tf_op jit(solution)/shard_map/ppermute | solution.py:29
  162.8 21.2 %collective-permute-start.4 = (bf16[2,128,3,512]{3,1,2,0:T(8,128)(2,1)S(1)}, bf16[2,128,3,512]{3,1,2,0:T(8,128)(2,1)S(1)}, u32[]{:S(2)}, u32[]{:S(2)}) collective-permute-start(bf16[2,128,3,512]{3,1,2,0:T(8,128)(2,1)S(1)} %collective-permute-done.3), channel_id=1, source_target_pairs={{0,8},{8,0},{16,24},{24,16},{32,40},{40,32},{48,56},{56,48},{64,72... | collective-permute-start | bytes 2359304 | tf_op jit(solution)/shard_map/ppermute | solution.py:29
  166.8 18.5 %collective-permute-start.6 = (bf16[2,128,3,512]{3,1,2,0:T(8,128)(2,1)S(1)}, bf16[2,128,3,512]{3,1,2,0:T(8,128)(2,1)S(1)}, u32[]{:S(2)}, u32[]{:S(2)}) collective-permute-start(bf16[2,128,3,512]{3,1,2,0:T(8,128)(2,1)S(1)} %collective-permute-done.5), channel_id=1, source_target_pairs={{0,8},{8,0},{16,24},{24,16},{32,40},{40,32},{48,56},{56,48},{64,72... | collective-permute-start | bytes 2359304 | tf_op jit(solution)/shard_map/ppermute | solution.py:29
  166.9 21.4 %collective-permute-start.8 = (bf16[2,128,3,512]{3,1,2,0:T(8,128)(2,1)S(1)}, bf16[2,128,3,512]{3,1,2,0:T(8,128)(2,1)S(1)}, u32[]{:S(2)}, u32[]{:S(2)}) collective-permute-start(bf16[2,128,3,512]{3,1,2,0:T(8,128)(2,1)S(1)} %collective-permute-done.7), channel_id=1, source_target_pairs={{0,8},{8,0},{16,24},{24,16},{32,40},{40,32},{48,56},{56,48},{64,72... | collective-permute-start | bytes 2359304 | tf_op jit(solution)/shard_map/ppermute | solution.py:29
  176.0 13.6 %collective-permute-start.10 = (bf16[2,128,3,512]{3,1,2,0:T(8,128)(2,1)S(1)}, bf16[2,128,3,512]{3,1,2,0:T(8,128)(2,1)S(1)}, u32[]{:S(2)}, u32[]{:S(2)}) collective-permute-start(bf16[2,128,3,512]{3,1,2,0:T(8,128)(2,1)S(1)} %collective-permute-done.9), channel_id=1, source_target_pairs={{0,8},{8,0},{16,24},{24,16},{32,40},{40,32},{48,56},{56,48},{64,72... | collective-permute-start | bytes 2359304 | tf_op jit(solution)/shard_map/ppermute | solution.py:29
  180.6 10.3 %collective-permute-start.14 = (bf16[2,128,3,512]{3,1,2,0:T(8,128)(2,1)S(1)}, bf16[2,128,3,512]{3,1,2,0:T(8,128)(2,1)S(1)}, u32[]{:S(2)}, u32[]{:S(2)}) collective-permute-start(bf16[2,128,3,512]{3,1,2,0:T(8,128)(2,1)S(1)} %collective-permute-done.13), channel_id=1, source_target_pairs={{0,8},{8,0},{16,24},{24,16},{32,40},{40,32},{48,56},{56,48},{64,72... | collective-permute-start | bytes 2359304 | tf_op jit(solution)/shard_map/ppermute | solution.py:29
  184.0 8.2 %collective-permute-start.15 = (bf16[2,128,3,512]{3,1,2,0:T(8,128)(2,1)S(1)}, bf16[2,128,3,512]{3,1,2,0:T(8,128)(2,1)S(1)}, u32[]{:S(2)}, u32[]{:S(2)}) collective-permute-start(bf16[2,128,3,512]{3,1,2,0:T(8,128)(2,1)S(1)} %collective-permute-done.12), channel_id=1, source_target_pairs={{0,8},{8,0},{16,24},{24,16},{32,40},{40,32},{48,56},{56,48},{64,72... | collective-permute-start | bytes 2359304 | tf_op jit(solution)/shard_map/ppermute | solution.py:29
  185.3 8.2 %collective-permute-start.16 = (bf16[2,128,3,512]{3,1,2,0:T(8,128)(2,1)S(1)}, bf16[2,128,3,512]{3,1,2,0:T(8,128)(2,1)S(1)}, u32[]{:S(2)}, u32[]{:S(2)}) collective-permute-start(bf16[2,128,3,512]{3,1,2,0:T(8,128)(2,1)S(1)} %collective-permute-done.11), channel_id=1, source_target_pairs={{0,8},{8,0},{16,24},{24,16},{32,40},{40,32},{48,56},{56,48},{64,72... | collective-permute-start | bytes 2359304 | tf_op jit(solution)/shard_map/ppermute | solution.py:29
  192.2 21.2 %copy-start.2 = (bf16[512,512]{1,0:T(8,128)(2,1)S(1)}, bf16[512,512]{1,0:T(8,128)(2,1)}, u32[]{:S(2)}) copy-start(bf16[512,512]{1,0:T(8,128)(2,1)} %param.10) | copy-start | bytes 1572868
  193.5 34.1 %copy-start.5 = (bf16[512]{0:T(512)(128)(2,1)S(1)}, bf16[512]{0:T(512)(128)(2,1)}, u32[]{:S(2)}) copy-start(bf16[512]{0:T(512)(128)(2,1)} %param.17) | copy-start | bytes 3076
  214.9 2.5 collective-permute-start.17
  217.4 3.9 %collective-permute-start.18 = (f32[512]{0:T(512)S(1)}, f32[512]{0:T(512)S(1)}, u32[]{:S(2)}, u32[]{:S(2)}) collective-permute-start(f32[512]{0:T(512)S(1)} %add.88), channel_id=1, source_target_pairs={{0,2},{1,3},{2,0},{3,1},{4,6},{5,7},{6,4},{7,5},{8,10},{9,11},{10,... | collective-permute-start | bytes 6152 | tf_op jit(solution)/shard_map/ppermute | solution.py:82
  221.3 3.9 %collective-permute-start.19 = (f32[512]{0:T(512)S(1)}, f32[512]{0:T(512)S(1)}, u32[]{:S(2)}, u32[]{:S(2)}) collective-permute-start(f32[512]{0:T(512)S(1)} %add.89), channel_id=1, source_target_pairs={{0,4},{1,5},{2,6},{3,7},{4,0},{5,1},{6,2},{7,3},{8,12},{9,13},{10,... | collective-permute-start | bytes 6152 | tf_op jit(solution)/shard_map/ppermute | solution.py:82
  337.1 13.3 %slice-start = ((bf16[512,1,512]{0,2,1:T(8,128)(2,1)}), bf16[384,1,512]{0,2,1:T(8,128)(2,1)S(1)}, s32[]{:S(2)}) async-start(bf16[512,1,512]{0,2,1:T(8,128)(2,1)} %fusion.21), calls=%async_computation.4 | async-start | bytes 786432 | tf_op jit(solution)/shard_map/slice | solution.py:151
  340.6 11.8 %collective-permute-start.20 = (bf16[128,32,16]{0,2,1:T(8,128)(2,1)}, bf16[128,32,16]{0,2,1:T(8,128)(2,1)}, u32[]{:S(2)}, u32[]{:S(2)}) collective-permute-start(bf16[128,32,16]{0,2,1:T(8,128)(2,1)} %bitcast.51), channel_id=1, source_target_pairs={{0,8},{8,16},{16,24},{24,32},{32,40},{40,48},{48,56},{56,64},{64,7... | collective-permute-start | bytes 393224 | tf_op jit(solution)/shard_map/ppermute | solution.py:17
  354.9 3.5 copy-start.1
Sparse Core Ops, SparseCore 0:
  9.2 66.7 all-gather.4
  93.8 119.5 reduce-scatter.1
  227.6 78.0 all-gather.6
where the time goes:
time: 366 us; the launch traced here: 365 us
  waiting for transfers between devices  220 us (60%)
  starting transfers between devices  44.5 us (12%)
  local copies, waits for them, and re-layouts  35.7 us (10%)
  matrix products  27.1 us (7%)
  other arithmetic  23.9 us (7%)
  between operations  13.4 us (4%)
    all_gather x1, waiting for transfers between devices, per_device(): gathered = lax.all_gather(normed, 'tp', axis=0, tiled=False)  74.7 us
    all_gather x1, waiting for transfers between devices, project_out(): stacked = lax.all_gather(w_out, 'seq', axis=0, tiled=False)  59.7 us
    ppermute x16, waiting for transfers between devices, exchange(): return lax.ppermute(block, axis, pairs)  59.4 us
    ppermute x16, starting transfers between devices, exchange(): return lax.ppermute(block, axis, pairs)  30.2 us
    reduce_scatter x1, waiting for transfers between devices, per_device(): lax.psum_scatter(partial_out, 'tp', scatter_dimension=0, tiled=True)[0]  18.7 us
    reshape x2, local copies, waits for them, and re-layouts, ring_features(): features = gathered.reshape(z_size, gathered.shape[1], 2, 2, rows)  12 us
    ppermute x2, starting transfers between devices, shifted(): return lax.ppermute(block, axis, route)  11.7 us
    dot_general x1, matrix products, per_device(): jnp.einsum('ktycr,kcyrin->tin', ring_features(gathered, w_in.shape[0]), w...  9.51 us
  transfers between devices with their start and end apart: 24, of which 11 were waited for; matrix products, arithmetic and copies ran while one was open for 6% of the time, Pallas kernels for 0%

commit v1 on v0

--- a/solution.py
+++ b/solution.py
@@ -126,7 +126,9 @@
     )
     gain_full = norm_gain.astype(jnp.float32)
     partial_out = project_out(y_se, w_out)
-    share = lax.psum_scatter(partial_out, "tp", scatter_dimension=0, tiled=True)[0]
+    share = lax.psum_scatter(
+        partial_out.astype(jnp.bfloat16), "tp", scatter_dimension=0, tiled=True
+    )[0].astype(jnp.float32)
     w_full = ring_rows(gather_rows(w_in))
     share, w_full = lax.optimization_barrier((share, w_full))
     stream = residual.astype(jnp.float32) + share

time: 366 us -> 342 us (0.934)
  waiting for transfers between devices: 220 us -> 198 us
    reduce_scatter x1, waiting for transfers between devices: 18.7 us -> 0.01 us  [per_device(): lax.psum_scatter(partial_out.astype(jnp.bfloat16), 'tp', scatter_dimensio...]
    reshape x1 -> x0, local copies, waits for them, and re-layouts: 9.14 us -> none  [project_out(): return partial.reshape(tp_size, y_se.shape[0], -1)]
    convert_element_type x0 -> x1, local copies, waits for them, and re-layouts: none -> 6.46 us  [per_device(): partial_out.astype(jnp.bfloat16)]
  transfers between devices with their start and end apart: 24 -> 24, of which waited for: 11 -> 10; matrix products, arithmetic and copies ran while one was open for 6% -> 7% of each run, Pallas kernels for 0% -> 0%
where the time goes in v1:
time: 342 us; the launch traced here: 341 us
  waiting for transfers between devices  198 us (58%)
  starting transfers between devices  47.6 us (14%)
  local copies, waits for them, and re-layouts  33 us (10%)
  matrix products  25.8 us (8%)
  other arithmetic  22.6 us (7%)
  between operations  13.4 us (4%)
    all_gather x1, waiting for transfers between devices, per_device(): gathered = lax.all_gather(normed, 'tp', axis=0, tiled=False)  74.3 us
    all_gather x1, waiting for transfers between devices, project_out(): stacked = lax.all_gather(w_out, 'seq', axis=0, tiled=False)  59.7 us
    ppermute x16, waiting for transfers between devices, exchange(): return lax.ppermute(block, axis, pairs)  59.6 us
    ppermute x16, starting transfers between devices, exchange(): return lax.ppermute(block, axis, pairs)  30.1 us
    reshape x2, local copies, waits for them, and re-layouts, ring_features(): features = gathered.reshape(z_size, gathered.shape[1], 2, 2, rows)  12 us
    ppermute x2, starting transfers between devices, shifted(): return lax.ppermute(block, axis, route)  11.7 us
    dot_general x1, matrix products, per_device(): jnp.einsum('ktycr,kcyrin->tin', ring_features(gathered, w_in.shape[0]), w...  9.51 us
    unnamed x7, other arithmetic  8.94 us
  transfers between devices with their start and end apart: 24, of which 10 were waited for; matrix products, arithmetic and copies ran while one was open for 7% of the time, Pallas kernels for 0%

profile of v1, /device:TPU:105, one launch (start us, length us, event | category | flops | bytes accessed | tf_op | source)
XLA Modules:
  0.0 340.8 jit_solution(13155461473353378037)
XLA Ops:
  8.7 5.2 %collective-permute-start = (bf16[6,512]{1,0:T(8,128)(2,1)S(1)}, bf16[6,512]{1,0:T(8,128)(2,1)S(1)}, u32[]{:S(2)}, u32[]{:S(2)}) collective-permute-start(bf16[6,512]{1,0:T(8,128)(2,1)S(1)} %slice_bitcast_fusion.1), channel_id=1, source_target_pairs={{0,8},{8,16},{16,24},{24,32},{32,40},{40,48},{48,56},{56,64},{64,7... | collective-permute-start | bytes 18440 | tf_op jit(solution)/shard_map/ppermute | solution.py:17
  16.3 59.7 %all-gather.5.cloned.1.call-done = bf16[16384,128]{1,0:T(8,128)(2,1)} async-done(((bf16[512,128]{1,0:T(8,128)(2,1)}), bf16[16384,128]{1,0:T(8,128)(2,1)}) %all-gather.5.cloned.1.call-update) | async-done | bytes 4194320 | tf_op jit(solution)/shard_map/all_gather | solution.py:103
  76.0 7.3 %convolution_convert_fusion = bf16[512,8,4,128]{0,3,2,1:T(8,128)(2,1)} fusion(bf16[8,4,512,128]{3,2,1,0:T(8,128)(2,1)} %bitcast.160, f32[518,512]{1,0:T(8,128)S(1)} %maximum_convert_fusion, f32[512]{0:T(512)S(1)} %convert_element_type.93, f32[512]{0:T(512)S(1)} %bitcast.154, f32[512]{0:T(512)S(1)} %bitcast.155, f32[512]{0:T(512)S(1)} %bitcast.156, ...), kind=kOutput, calls=%fused_computation.10 | convolution fusion | flops 2154561536 | bytes 16793600 | tf_op jit(solution)/shard_map/tc,kjcf->ktjf/dot_general | solution.py:105
  83.3 6.5 %copy.31 = bf16[8,512,512]{2,1,0:T(8,128)(2,1)} copy(bf16[8,512,512]{1,2,0:T(8,128)(2,1)} %bitcast.136) | data formatting | bytes 8388608 | tf_op jit(solution)/shard_map/convert_element_type | solution.py:130
  92.0 9.1 %collective-permute-done.1 = bf16[128,3,512]{2,0,1:T(8,128)(2,1)S(1)} collective-permute-done((bf16[128,3,512]{2,0,1:T(8,128)(2,1)S(1)}, bf16[128,3,512]{2,0,1:T(8,128)(2,1)S(1)}, u32[]{:S(2)}, u32[]{:S(2)}) %collective-permute-start.1) | collective-permute-done | bytes 393248 | tf_op jit(solution)/shard_map/ppermute | solution.py:29
  101.3 2.6 collective-permute-start.3
  103.9 15.8 %collective-permute-done.3 = bf16[2,128,3,512]{3,1,2,0:T(8,128)(2,1)S(1)} collective-permute-done((bf16[2,128,3,512]{3,1,2,0:T(8,128)(2,1)S(1)}, bf16[2,128,3,512]{3,1,2,0:T(8,128)(2,1)S(1)}, u32[]{:S(2)}, u32[]{:S(2)}) %collective-permute-start.3) | collective-permute-done | bytes 786464 | tf_op jit(solution)/shard_map/ppermute | solution.py:29
  119.7 3.4 %collective-permute-start.5 = (bf16[2,128,3,512]{3,1,2,0:T(8,128)(2,1)S(1)}, bf16[2,128,3,512]{3,1,2,0:T(8,128)(2,1)S(1)}, u32[]{:S(2)}, u32[]{:S(2)}) collective-permute-start(bf16[2,128,3,512]{3,1,2,0:T(8,128)(2,1)S(1)} %collective-permute-done.3), channel_id=1, source_target_pairs={{0,32},{8,40},{16,48},{24,56},{32,64},{40,72},{48,80},{56,88},{64,... | collective-permute-start | bytes 2359304 | tf_op jit(solution)/shard_map/ppermute | solution.py:29
  123.1 14.9 %collective-permute-done.5 = bf16[2,128,3,512]{3,1,2,0:T(8,128)(2,1)S(1)} collective-permute-done((bf16[2,128,3,512]{3,1,2,0:T(8,128)(2,1)S(1)}, bf16[2,128,3,512]{3,1,2,0:T(8,128)(2,1)S(1)}, u32[]{:S(2)}, u32[]{:S(2)}) %collective-permute-start.5) | collective-permute-done | bytes 786464 | tf_op jit(solution)/shard_map/ppermute | solution.py:29
  138.0 3.5 %collective-permute-start.7 = (bf16[2,128,3,512]{3,1,2,0:T(8,128)(2,1)S(1)}, bf16[2,128,3,512]{3,1,2,0:T(8,128)(2,1)S(1)}, u32[]{:S(2)}, u32[]{:S(2)}) collective-permute-start(bf16[2,128,3,512]{3,1,2,0:T(8,128)(2,1)S(1)} %collective-permute-done.5), channel_id=1, source_target_pairs={{0,32},{8,40},{16,48},{24,56},{32,64},{40,72},{48,80},{56,88},{64,... | collective-permute-start | bytes 2359304 | tf_op jit(solution)/shard_map/ppermute | solution.py:29
  141.5 3.1 collective-permute-start.2
  144.5 11.0 %collective-permute-done.7 = bf16[2,128,3,512]{3,1,2,0:T(8,128)(2,1)S(1)} collective-permute-done((bf16[2,128,3,512]{3,1,2,0:T(8,128)(2,1)S(1)}, bf16[2,128,3,512]{3,1,2,0:T(8,128)(2,1)S(1)}, u32[]{:S(2)}, u32[]{:S(2)}) %collective-permute-start.7) | collective-permute-done | bytes 786464 | tf_op jit(solution)/shard_map/ppermute | solution.py:29
  155.6 3.4 %collective-permute-start.9 = (bf16[2,128,3,512]{3,1,2,0:T(8,128)(2,1)S(1)}, bf16[2,128,3,512]{3,1,2,0:T(8,128)(2,1)S(1)}, u32[]{:S(2)}, u32[]{:S(2)}) collective-permute-start(bf16[2,128,3,512]{3,1,2,0:T(8,128)(2,1)S(1)} %collective-permute-done.7), channel_id=1, source_target_pairs={{0,32},{8,40},{16,48},{24,56},{32,64},{40,72},{48,80},{56,88},{64,... | collective-permute-start | bytes 2359304 | tf_op jit(solution)/shard_map/ppermute | solution.py:29
  159.0 3.9 %collective-permute-start.4 = (bf16[2,128,3,512]{3,1,2,0:T(8,128)(2,1)S(1)}, bf16[2,128,3,512]{3,1,2,0:T(8,128)(2,1)S(1)}, u32[]{:S(2)}, u32[]{:S(2)}) collective-permute-start(bf16[2,128,3,512]{3,1,2,0:T(8,128)(2,1)S(1)} %collective-permute-done.3), channel_id=1, source_target_pairs={{0,8},{8,0},{16,24},{24,16},{32,40},{40,32},{48,56},{56,48},{64,72... | collective-permute-start | bytes 2359304 | tf_op jit(solution)/shard_map/ppermute | solution.py:29
  163.4 8.8 %collective-permute-done.9 = bf16[2,128,3,512]{3,1,2,0:T(8,128)(2,1)S(1)} collective-permute-done((bf16[2,128,3,512]{3,1,2,0:T(8,128)(2,1)S(1)}, bf16[2,128,3,512]{3,1,2,0:T(8,128)(2,1)S(1)}, u32[]{:S(2)}, u32[]{:S(2)}) %collective-permute-start.9) | collective-permute-done | bytes 786464 | tf_op jit(solution)/shard_map/ppermute | solution.py:29
  172.2 4.5 %collective-permute-start.10 = (bf16[2,128,3,512]{3,1,2,0:T(8,128)(2,1)S(1)}, bf16[2,128,3,512]{3,1,2,0:T(8,128)(2,1)S(1)}, u32[]{:S(2)}, u32[]{:S(2)}) collective-permute-start(bf16[2,128,3,512]{3,1,2,0:T(8,128)(2,1)S(1)} %collective-permute-done.9), channel_id=1, source_target_pairs={{0,8},{8,0},{16,24},{24,16},{32,40},{40,32},{48,56},{56,48},{64,72... | collective-permute-start | bytes 2359304 | tf_op jit(solution)/shard_map/ppermute | solution.py:29
  176.7 3.4 %collective-permute-start.14 = (bf16[2,128,3,512]{3,1,2,0:T(8,128)(2,1)S(1)}, bf16[2,128,3,512]{3,1,2,0:T(8,128)(2,1)S(1)}, u32[]{:S(2)}, u32[]{:S(2)}) collective-permute-start(bf16[2,128,3,512]{3,1,2,0:T(8,128)(2,1)S(1)} %collective-permute-done.13), channel_id=1, source_target_pairs={{0,8},{8,0},{16,24},{24,16},{32,40},{40,32},{48,56},{56,48},{64,72... | collective-permute-start | bytes 2359304 | tf_op jit(solution)/shard_map/ppermute | solution.py:29
  194.8 2.8 collective-permute-start.18
  198.8 1.9 collective-permute-start.19
  203.9 3.4 select_bitcast_fusion
  207.2 74.3 %all-gather.7.cloned.1.call-done = bf16[4096,512]{1,0:T(8,128)(2,1)} async-done(((bf16[512,512]{1,0:T(8,128)(2,1)}), bf16[4096,512]{1,0:T(8,128)(2,1)}) %all-gather.7.cloned.1.call-update) | async-done | bytes 4194320 | tf_op jit(solution)/shard_map/all_gather | solution.py:139
  281.6 6.9 %reshape.82 = bf16[8,512,2,2,128]{4,3,2,1,0:T(2,128)(2,1)} reshape(bf16[4096,512]{1,0:T(8,128)(2,1)} %all-gather.7.cloned.1.call-done) | data formatting | bytes 8388608 | tf_op jit(solution)/shard_map/reshape | solution.py:69
  288.5 5.1 %copy.32 = bf16[8,512,2,2,128]{4,1,2,0,3:T(8,128)(2,1)} copy(bf16[8,512,2,2,128]{4,3,2,1,0:T(2,128)(2,1)} %reshape.82) | data formatting | bytes 8388608 | tf_op jit(solution)/shard_map/reshape | solution.py:69
  293.6 4.6 %rev.6 = bf16[8,512,2,2,128]{4,1,2,0,3:T(8,128)(2,1)} reverse(bf16[8,512,2,2,128]{4,1,2,0,3:T(8,128)(2,1)} %copy.32), dimensions={0} | reverse | bytes 8388608 | tf_op jit(solution)/shard_map/rev | solution.py:70
  298.2 3.1 fusion.4
  302.4 9.5 %fusion.6 = f32[512,3,512]{0,2,1:T(8,128)S(1)} fusion(bf16[8,512,2,2,128,1]{4,1,2,5,0,3:T(8,128)(2,1)S(1)} %fusion.3, bf16[8,2,2,128,3,512]{5,3,4,2,1,0:T(8,128)(2,1)} %fusion.16), kind=kOutput, calls=%fused_computation.11 | convolution fusion | flops 6442450944 | bytes 19922944 | tf_op jit(solution)/shard_map/ktycr,kcyrin->tin/dot_general | solution.py:140
  312.9 2.0 convert_element_type.104
  314.9 1.6 slice.121
  316.5 6.5 %collective-permute-start.20 = (bf16[128,32,16]{0,2,1:T(8,128)(2,1)}, bf16[128,32,16]{0,2,1:T(8,128)(2,1)}, u32[]{:S(2)}, u32[]{:S(2)}) collective-permute-start(bf16[128,32,16]{0,2,1:T(8,128)(2,1)} %bitcast.51), channel_id=1, source_target_pairs={{0,8},{8,16},{16,24},{24,32},{32,40},{40,48},{48,56},{56,64},{64,7... | collective-permute-start | bytes 393224 | tf_op jit(solution)/shard_map/ppermute | solution.py:17
  323.0 3.2 fusion.32
  328.2 2.5 fusion.18
  332.2 2.0 copy.39
  (80 shorter events, 31.9 us)
Async XLA Ops:
  6.5 197.3 %copy-start = (bf16[32,128]{1,0:T(8,128)(2,1)S(1)}, bf16[32,128]{1,0:T(8,128)(2,1)}, u32[]{:S(2)}) copy-start(bf16[32,128]{1,0:T(8,128)(2,1)} %param.16) | copy-start | bytes 24580
  6.5 9.6 %copy-start.4 = (bf16[512]{0:T(512)(128)(2,1)S(1)}, bf16[512]{0:T(512)(128)(2,1)}, u32[]{:S(2)}) copy-start(bf16[512]{0:T(512)(128)(2,1)} %param.12) | copy-start | bytes 3076
  6.5 69.5 %all-gather.5.cloned.1.call-start = ((), (), s32[]{:S(2)}) async-start(), calls=%async_computation.2 | async-start | bytes 4325376 | tf_op jit(solution)/shard_map/all_gather | solution.py:103
  7.3 183.6 %reduce-scatter.2.cloned.1.call-start = ((), (), s32[]{:S(2)}) async-start(), calls=%async_computation.1 | async-start | bytes 4718592 | tf_op jit(solution)/shard_map/reduce_scatter | solution.py:129
  8.7 7.5 %collective-permute-start = (bf16[6,512]{1,0:T(8,128)(2,1)S(1)}, bf16[6,512]{1,0:T(8,128)(2,1)S(1)}, u32[]{:S(2)}, u32[]{:S(2)}) collective-permute-start(bf16[6,512]{1,0:T(8,128)(2,1)S(1)} %slice_bitcast_fusion.1), channel_id=1, source_target_pairs={{0,8},{8,16},{16,24},{24,32},{32,40},{40,48},{48,56},{56,64},{64,7... | collective-permute-start | bytes 18440 | tf_op jit(solution)/shard_map/ppermute | solution.py:17
  89.7 1.0 copy-start.3
  89.8 191.8 %all-gather.7.cloned.1.call-start = ((), (), s32[]{:S(2)}) async-start(), calls=%async_computation.3 | async-start | bytes 4718592 | tf_op jit(solution)/shard_map/all_gather | solution.py:139
  90.7 10.4 %collective-permute-start.1 = (bf16[128,3,512]{2,0,1:T(8,128)(2,1)S(1)}, bf16[128,3,512]{2,0,1:T(8,128)(2,1)S(1)}, u32[]{:S(2)}, u32[]{:S(2)}) collective-permute-start(bf16[128,3,512]{2,0,1:T(8,128)(2,1)S(1)} %copy-done.3), channel_id=1, source_target_pairs={{0,16},{8,24},{16,0},{24,8},{32,48},{40,56},{48,32},{56,40},{64,80... | collective-permute-start | bytes 1179656 | tf_op jit(solution)/shard_map/ppermute | solution.py:29
  101.3 18.4 %collective-permute-start.3 = (bf16[2,128,3,512]{3,1,2,0:T(8,128)(2,1)S(1)}, bf16[2,128,3,512]{3,1,2,0:T(8,128)(2,1)S(1)}, u32[]{:S(2)}, u32[]{:S(2)}) collective-permute-start(bf16[2,128,3,512]{3,1,2,0:T(8,128)(2,1)S(1)} %get-tuple-element.12), channel_id=1, source_target_pairs={{0,32},{8,40},{16,48},{24,56},{32,64},{40,72},{48,80},{56,88},{64,... | collective-permute-start | bytes 2359304 | tf_op jit(solution)/shard_map/ppermute | solution.py:29
  119.7 18.3 %collective-permute-start.5 = (bf16[2,128,3,512]{3,1,2,0:T(8,128)(2,1)S(1)}, bf16[2,128,3,512]{3,1,2,0:T(8,128)(2,1)S(1)}, u32[]{:S(2)}, u32[]{:S(2)}) collective-permute-start(bf16[2,128,3,512]{3,1,2,0:T(8,128)(2,1)S(1)} %collective-permute-done.3), channel_id=1, source_target_pairs={{0,32},{8,40},{16,48},{24,56},{32,64},{40,72},{48,80},{56,88},{64,... | collective-permute-start | bytes 2359304 | tf_op jit(solution)/shard_map/ppermute | solution.py:29
  123.1 18.4 %collective-permute-start.11 = (bf16[2,128,3,512]{3,1,2,0:T(8,128)(2,1)S(1)}, bf16[2,128,3,512]{3,1,2,0:T(8,128)(2,1)S(1)}, u32[]{:S(2)}, u32[]{:S(2)}) collective-permute-start(bf16[2,128,3,512]{3,1,2,0:T(8,128)(2,1)S(1)} %get-tuple-element.12), channel_id=1, source_target_pairs={{0,224},{8,232},{16,240},{24,248},{32,0},{40,8},{48,16},{56,24},{6... | collective-permute-start | bytes 2359304 | tf_op jit(solution)/shard_map/ppermute | solution.py:29
  138.0 17.6 %collective-permute-start.7 = (bf16[2,128,3,512]{3,1,2,0:T(8,128)(2,1)S(1)}, bf16[2,128,3,512]{3,1,2,0:T(8,128)(2,1)S(1)}, u32[]{:S(2)}, u32[]{:S(2)}) collective-permute-start(bf16[2,128,3,512]{3,1,2,0:T(8,128)(2,1)S(1)} %collective-permute-done.5), channel_id=1, source_target_pairs={{0,32},{8,40},{16,48},{24,56},{32,64},{40,72},{48,80},{56,88},{64,... | collective-permute-start | bytes 2359304 | tf_op jit(solution)/shard_map/ppermute | solution.py:29
  141.5 17.5 %collective-permute-start.12 = (bf16[2,128,3,512]{3,1,2,0:T(8,128)(2,1)S(1)}, bf16[2,128,3,512]{3,1,2,0:T(8,128)(2,1)S(1)}, u32[]{:S(2)}, u32[]{:S(2)}) collective-permute-start(bf16[2,128,3,512]{3,1,2,0:T(8,128)(2,1)S(1)} %collective-permute-done.11), channel_id=1, source_target_pairs={{0,224},{8,232},{16,240},{24,248},{32,0},{40,8},{48,16},{56,24},{6... | collective-permute-start | bytes 2359304 | tf_op jit(solution)/shard_map/ppermute | solution.py:29
  141.5 21.5 %collective-permute-start.2 = (bf16[2,128,3,512]{3,1,2,0:T(8,128)(2,1)S(1)}, bf16[2,128,3,512]{3,1,2,0:T(8,128)(2,1)S(1)}, u32[]{:S(2)}, u32[]{:S(2)}) collective-permute-start(bf16[2,128,3,512]{3,1,2,0:T(8,128)(2,1)S(1)} %get-tuple-element.12), channel_id=1, source_target_pairs={{0,8},{8,0},{16,24},{24,16},{32,40},{40,32},{48,56},{56,48},{64,72... | collective-permute-start | bytes 2359304 | tf_op jit(solution)/shard_map/ppermute | solution.py:29
  155.6 16.7 %collective-permute-start.9 = (bf16[2,128,3,512]{3,1,2,0:T(8,128)(2,1)S(1)}, bf16[2,128,3,512]{3,1,2,0:T(8,128)(2,1)S(1)}, u32[]{:S(2)}, u32[]{:S(2)}) collective-permute-start(bf16[2,128,3,512]{3,1,2,0:T(8,128)(2,1)S(1)} %collective-permute-done.7), channel_id=1, source_target_pairs={{0,32},{8,40},{16,48},{24,56},{32,64},{40,72},{48,80},{56,88},{64,... | collective-permute-start | bytes 2359304 | tf_op jit(solution)/shard_map/ppermute | solution.py:29
  159.0 17.8 %collective-permute-start.13 = (bf16[2,128,3,512]{3,1,2,0:T(8,128)(2,1)S(1)}, bf16[2,128,3,512]{3,1,2,0:T(8,128)(2,1)S(1)}, u32[]{:S(2)}, u32[]{:S(2)}) collective-permute-start(bf16[2,128,3,512]{3,1,2,0:T(8,128)(2,1)S(1)} %collective-permute-done.12), channel_id=1, source_target_pairs={{0,224},{8,232},{16,240},{24,248},{32,0},{40,8},{48,16},{56,24},{6... | collective-permute-start | bytes 2359304 | tf_op jit(solution)/shard_map/ppermute | solution.py:29
  159.0 21.2 %collective-permute-start.4 = (bf16[2,128,3,512]{3,1,2,0:T(8,128)(2,1)S(1)}, bf16[2,128,3,512]{3,1,2,0:T(8,128)(2,1)S(1)}, u32[]{:S(2)}, u32[]{:S(2)}) collective-permute-start(bf16[2,128,3,512]{3,1,2,0:T(8,128)(2,1)S(1)} %collective-permute-done.3), channel_id=1, source_target_pairs={{0,8},{8,0},{16,24},{24,16},{32,40},{40,32},{48,56},{56,48},{64,72... | collective-permute-start | bytes 2359304 | tf_op jit(solution)/shard_map/ppermute | solution.py:29
  162.9 18.5 %collective-permute-start.6 = (bf16[2,128,3,512]{3,1,2,0:T(8,128)(2,1)S(1)}, bf16[2,128,3,512]{3,1,2,0:T(8,128)(2,1)S(1)}, u32[]{:S(2)}, u32[]{:S(2)}) collective-permute-start(bf16[2,128,3,512]{3,1,2,0:T(8,128)(2,1)S(1)} %collective-permute-done.5), channel_id=1, source_target_pairs={{0,8},{8,0},{16,24},{24,16},{32,40},{40,32},{48,56},{56,48},{64,72... | collective-permute-start | bytes 2359304 | tf_op jit(solution)/shard_map/ppermute | solution.py:29
  163.0 21.4 %collective-permute-start.8 = (bf16[2,128,3,512]{3,1,2,0:T(8,128)(2,1)S(1)}, bf16[2,128,3,512]{3,1,2,0:T(8,128)(2,1)S(1)}, u32[]{:S(2)}, u32[]{:S(2)}) collective-permute-start(bf16[2,128,3,512]{3,1,2,0:T(8,128)(2,1)S(1)} %collective-permute-done.7), channel_id=1, source_target_pairs={{0,8},{8,0},{16,24},{24,16},{32,40},{40,32},{48,56},{56,48},{64,72... | collective-permute-start | bytes 2359304 | tf_op jit(solution)/shard_map/ppermute | solution.py:29
  172.2 13.6 %collective-permute-start.10 = (bf16[2,128,3,512]{3,1,2,0:T(8,128)(2,1)S(1)}, bf16[2,128,3,512]{3,1,2,0:T(8,128)(2,1)S(1)}, u32[]{:S(2)}, u32[]{:S(2)}) collective-permute-start(bf16[2,128,3,512]{3,1,2,0:T(8,128)(2,1)S(1)} %collective-permute-done.9), channel_id=1, source_target_pairs={{0,8},{8,0},{16,24},{24,16},{32,40},{40,32},{48,56},{56,48},{64,72... | collective-permute-start | bytes 2359304 | tf_op jit(solution)/shard_map/ppermute | solution.py:29
  176.7 10.3 %collective-permute-start.14 = (bf16[2,128,3,512]{3,1,2,0:T(8,128)(2,1)S(1)}, bf16[2,128,3,512]{3,1,2,0:T(8,128)(2,1)S(1)}, u32[]{:S(2)}, u32[]{:S(2)}) collective-permute-start(bf16[2,128,3,512]{3,1,2,0:T(8,128)(2,1)S(1)} %collective-permute-done.13), channel_id=1, source_target_pairs={{0,8},{8,0},{16,24},{24,16},{32,40},{40,32},{48,56},{56,48},{64,72... | collective-permute-start | bytes 2359304 | tf_op jit(solution)/shard_map/ppermute | solution.py:29
  180.1 8.2 %collective-permute-start.15 = (bf16[2,128,3,512]{3,1,2,0:T(8,128)(2,1)S(1)}, bf16[2,128,3,512]{3,1,2,0:T(8,128)(2,1)S(1)}, u32[]{:S(2)}, u32[]{:S(2)}) collective-permute-start(bf16[2,128,3,512]{3,1,2,0:T(8,128)(2,1)S(1)} %collective-permute-done.12), channel_id=1, source_target_pairs={{0,8},{8,0},{16,24},{24,16},{32,40},{40,32},{48,56},{56,48},{64,72... | collective-permute-start | bytes 2359304 | tf_op jit(solution)/shard_map/ppermute | solution.py:29
  181.4 8.2 %collective-permute-start.16 = (bf16[2,128,3,512]{3,1,2,0:T(8,128)(2,1)S(1)}, bf16[2,128,3,512]{3,1,2,0:T(8,128)(2,1)S(1)}, u32[]{:S(2)}, u32[]{:S(2)}) collective-permute-start(bf16[2,128,3,512]{3,1,2,0:T(8,128)(2,1)S(1)} %collective-permute-done.11), channel_id=1, source_target_pairs={{0,8},{8,0},{16,24},{24,16},{32,40},{40,32},{48,56},{56,48},{64,72... | collective-permute-start | bytes 2359304 | tf_op jit(solution)/shard_map/ppermute | solution.py:29
  189.6 2.5 copy-start.2
  190.9 12.9 %copy-start.5 = (bf16[512]{0:T(512)(128)(2,1)S(1)}, bf16[512]{0:T(512)(128)(2,1)}, u32[]{:S(2)}) copy-start(bf16[512]{0:T(512)(128)(2,1)} %param.17) | copy-start | bytes 3076
  192.3 2.5 collective-permute-start.17
  194.8 3.9 %collective-permute-start.18 = (f32[512]{0:T(512)S(1)}, f32[512]{0:T(512)S(1)}, u32[]{:S(2)}, u32[]{:S(2)}) collective-permute-start(f32[512]{0:T(512)S(1)} %add.88), channel_id=1, source_target_pairs={{0,2},{1,3},{2,0},{3,1},{4,6},{5,7},{6,4},{7,5},{8,10},{9,11},{10,... | collective-permute-start | bytes 6152 | tf_op jit(solution)/shard_map/ppermute | solution.py:82
  198.8 3.9 %collective-permute-start.19 = (f32[512]{0:T(512)S(1)}, f32[512]{0:T(512)S(1)}, u32[]{:S(2)}, u32[]{:S(2)}) collective-permute-start(f32[512]{0:T(512)S(1)} %add.89), channel_id=1, source_target_pairs={{0,4},{1,5},{2,6},{3,7},{4,0},{5,1},{6,2},{7,3},{8,12},{9,13},{10,... | collective-permute-start | bytes 6152 | tf_op jit(solution)/shard_map/ppermute | solution.py:82
  312.9 13.3 %slice-start = ((bf16[512,1,512]{0,2,1:T(8,128)(2,1)}), bf16[384,1,512]{0,2,1:T(8,128)(2,1)S(1)}, s32[]{:S(2)}) async-start(bf16[512,1,512]{0,2,1:T(8,128)(2,1)} %fusion.21), calls=%async_computation.4 | async-start | bytes 786432 | tf_op jit(solution)/shard_map/slice | solution.py:153
  316.5 11.8 %collective-permute-start.20 = (bf16[128,32,16]{0,2,1:T(8,128)(2,1)}, bf16[128,32,16]{0,2,1:T(8,128)(2,1)}, u32[]{:S(2)}, u32[]{:S(2)}) collective-permute-start(bf16[128,32,16]{0,2,1:T(8,128)(2,1)} %bitcast.51), channel_id=1, source_target_pairs={{0,8},{8,16},{16,24},{24,32},{32,40},{40,48},{48,56},{56,64},{64,7... | collective-permute-start | bytes 393224 | tf_op jit(solution)/shard_map/ppermute | solution.py:17
  330.7 3.5 %copy-start.1 = (bf16[32,128]{1,0:T(8,128)(2,1)S(1)}, bf16[32,128]{1,0:T(8,128)(2,1)}, u32[]{:S(2)}) copy-start(bf16[32,128]{1,0:T(8,128)(2,1)} %param.16) | copy-start | bytes 24580
Sparse Core Ops, SparseCore 0:
  9.2 66.7 all-gather.4
  89.9 89.5 reduce-scatter.1
  203.8 77.6 all-gather.6

commit v2 on v0

--- a/solution.py
+++ b/solution.py
@@ -57,21 +57,22 @@
     return [(k, mine, exchange(mine, "seq", core_pair)) for k, mine in blocks]
 
 
-def ring_rows(pieces):
-    return jnp.stack([jnp.stack([mine, partner]) for _, mine, partner in sorted(pieces)])
-
-
-def ring_features(gathered, rows):
-    z_size = gathered.shape[0]
+def absolute_rows(pieces):
     me = lax.axis_index("seq")
     my_z = me // 4
-    my_core = me % 2
-    features = gathered.reshape(z_size, gathered.shape[1], 2, 2, rows)
-    reverse = features[::-1]
+    mine_first = me % 2 == 0
+    by_offset = jnp.stack(
+        [
+            jnp.where(
+                mine_first, jnp.stack([mine, partner], axis=1), jnp.stack([partner, mine], axis=1)
+            )
+            for _, mine, partner in sorted(pieces)
+        ]
+    )
+    z_size = by_offset.shape[0]
+    reverse = by_offset[::-1]
     doubled = jnp.concatenate([reverse, reverse], axis=0)
-    start = (z_size - 1 - my_z) % z_size
-    by_offset = lax.dynamic_slice_in_dim(doubled, start, z_size, axis=0)
-    return jnp.where(my_core == 0, by_offset, by_offset[:, :, :, ::-1])
+    return lax.dynamic_slice_in_dim(doubled, (z_size - 1 - my_z) % z_size, z_size, axis=0)
 
 
 def tp_sum(value):
@@ -127,7 +128,7 @@
     gain_full = norm_gain.astype(jnp.float32)
     partial_out = project_out(y_se, w_out)
     share = lax.psum_scatter(partial_out, "tp", scatter_dimension=0, tiled=True)[0]
-    w_full = ring_rows(gather_rows(w_in))
+    w_full = absolute_rows(gather_rows(w_in))
     share, w_full = lax.optimization_barrier((share, w_full))
     stream = residual.astype(jnp.float32) + share
     squares = tp_sum(jnp.sum(stream * stream, axis=1))
@@ -136,9 +137,9 @@
     normed = (stream * scale[:, None] * my_gain).astype(jnp.bfloat16)
     gathered = lax.all_gather(normed, "tp", axis=0, tiled=False)
     proj = jnp.einsum(
-        "ktycr,kcyrin->tin",
-        ring_features(gathered, w_in.shape[0]),
-        w_full,
+        "ktf,kfin->tin",
+        gathered,
+        w_full.reshape(gathered.shape[0], gathered.shape[2], *w_in.shape[1:]),
         preferred_element_type=jnp.float32,
     )
     query_mr = proj[:, 0]

time: 366 us -> 362 us (0.989)
  other arithmetic: 23.9 us -> 41.3 us
  waiting for transfers between devices: 220 us -> 204 us
  local copies, waits for them, and re-layouts: 35.7 us -> 29.8 us
    reduce_scatter x1, waiting for transfers between devices: 18.7 us -> 0.01 us  [per_device(): lax.psum_scatter(partial_out, 'tp', scatter_dimension=0, tiled=True)[0]]
    reshape x2 -> x0, local copies, waits for them, and re-layouts: 12 us -> none  [ring_features(): features = gathered.reshape(z_size, gathered.shape[1], 2, 2, rows)]
    unnamed x7, other arithmetic: 8.94 us -> 20.4 us
    concatenate x1, other arithmetic: 3.07 us -> 12.2 us  [absolute_rows(): doubled = jnp.concatenate([reverse, reverse], axis=0)]
    rev x1, local copies, waits for them, and re-layouts: 4.61 us -> 10.7 us  [absolute_rows(): reverse = by_offset[::-1]]
  transfers between devices with their start and end apart: 24 -> 24, of which waited for: 11 -> 12; matrix products, arithmetic and copies ran while one was open for 6% -> 16% of each run, Pallas kernels for 0% -> 0%
where the time goes in v2:
time: 362 us; the launch traced here: 361 us
  waiting for transfers between devices  204 us (56%)
  starting transfers between devices  44.7 us (12%)
  other arithmetic  41.3 us (11%)
  local copies, waits for them, and re-layouts  29.8 us (8%)
  matrix products  28.1 us (8%)
  between operations  13.4 us (4%)
    all_gather x1, waiting for transfers between devices, per_device(): gathered = lax.all_gather(normed, 'tp', axis=0, tiled=False)  74.3 us
    ppermute x16, waiting for transfers between devices, exchange(): return lax.ppermute(block, axis, pairs)  62.8 us
    all_gather x1, waiting for transfers between devices, project_out(): stacked = lax.all_gather(w_out, 'seq', axis=0, tiled=False)  61.2 us
    ppermute x16, starting transfers between devices, exchange(): return lax.ppermute(block, axis, pairs)  27.3 us
    unnamed x7, other arithmetic  20.4 us
    concatenate x1, other arithmetic, absolute_rows(): doubled = jnp.concatenate([reverse, reverse], axis=0)  12.2 us
    ppermute x2, starting transfers between devices, shifted(): return lax.ppermute(block, axis, route)  11.7 us
    rev x1, local copies, waits for them, and re-layouts, absolute_rows(): reverse = by_offset[::-1]  10.7 us
  transfers between devices with their start and end apart: 24, of which 12 were waited for; matrix products, arithmetic and copies ran while one was open for 16% of the time, Pallas kernels for 0%

profile of v2, /device:TPU:105, one launch (start us, length us, event | category | flops | bytes accessed | tf_op | source)
XLA Modules:
  0.0 360.8 jit_solution(3801346780649440677)
XLA Ops:
  8.7 5.2 %collective-permute-start = (bf16[6,512]{1,0:T(8,128)(2,1)S(1)}, bf16[6,512]{1,0:T(8,128)(2,1)S(1)}, u32[]{:S(2)}, u32[]{:S(2)}) collective-permute-start(bf16[6,512]{1,0:T(8,128)(2,1)S(1)} %slice_bitcast_fusion.1), channel_id=1, source_target_pairs={{0,8},{8,16},{16,24},{24,32},{32,40},{40,48},{48,56},{56,64},{64,7... | collective-permute-start | bytes 18440 | tf_op jit(solution)/shard_map/ppermute | solution.py:17
  14.8 61.2 %all-gather.5.cloned.1.call-done = bf16[16384,128]{1,0:T(8,128)(2,1)} async-done(((bf16[512,128]{1,0:T(8,128)(2,1)}), bf16[16384,128]{1,0:T(8,128)(2,1)}) %all-gather.5.cloned.1.call-update) | async-done | bytes 4194320 | tf_op jit(solution)/shard_map/all_gather | solution.py:104
  76.0 8.4 %fusion.24 = f32[512,8,4,128]{0,3,2,1:T(8,128)} fusion(bf16[8,4,512,128]{3,2,1,0:T(8,128)(2,1)} %bitcast.128, f32[518,512]{1,0:T(8,128)S(1)} %maximum_convert_fusion, f32[512]{0:T(512)S(1)} %convert_element_type.78, f32[512]{0:T(512)S(1)} %bitcast.122, f32[512]{0:T(512)S(1)} %bitcast.123, f32[512]{0:T(512)S(1)} %bitcast.124, f32[512]{0:T(512)S(1)} %bitcast.125, ...), kind=kOutput, calls=%fused_computation.63 | convolution fusion | flops 2152464384 | bytes 20987904 | tf_op jit(solution)/shard_map/tc,kjcf->ktjf/dot_general | solution.py:106
  84.4 9.1 %copy.37 = f32[8,512,512]{2,1,0:T(8,128)} copy(f32[8,512,512]{1,2,0:T(8,128)} %bitcast.109) | data formatting | bytes 16777216 | tf_op jit(solution)/shard_map/reshape | solution.py:107
  95.8 9.1 %collective-permute-done.1 = bf16[128,3,512]{2,0,1:T(8,128)(2,1)S(1)} collective-permute-done((bf16[128,3,512]{2,0,1:T(8,128)(2,1)S(1)}, bf16[128,3,512]{2,0,1:T(8,128)(2,1)S(1)}, u32[]{:S(2)}, u32[]{:S(2)}) %collective-permute-start.1) | collective-permute-done | bytes 393248 | tf_op jit(solution)/shard_map/ppermute | solution.py:29
  105.1 2.6 collective-permute-start.3
  107.7 15.8 %collective-permute-done.3 = bf16[2,128,3,512]{3,1,0,2:T(8,128)(2,1)} collective-permute-done((bf16[2,128,3,512]{3,1,0,2:T(8,128)(2,1)S(1)}, bf16[2,128,3,512]{3,1,0,2:T(8,128)(2,1)}, u32[]{:S(2)}, u32[]{:S(2)}) %collective-permute-start.3) | collective-permute-done | bytes 786464 | tf_op jit(solution)/shard_map/ppermute | solution.py:29
  123.5 3.5 collective-permute-start.5
  127.0 15.2 %collective-permute-done.5 = bf16[2,128,3,512]{3,1,0,2:T(8,128)(2,1)S(1)} collective-permute-done((bf16[2,128,3,512]{3,1,0,2:T(8,128)(2,1)}, bf16[2,128,3,512]{3,1,0,2:T(8,128)(2,1)S(1)}, u32[]{:S(2)}, u32[]{:S(2)}) %collective-permute-start.5) | collective-permute-done | bytes 786464 | tf_op jit(solution)/shard_map/ppermute | solution.py:29
  142.2 3.4 collective-permute-start.7
  145.6 3.0 collective-permute-start.2
  148.7 11.1 %collective-permute-done.7 = bf16[2,128,3,512]{3,1,0,2:T(8,128)(2,1)} collective-permute-done((bf16[2,128,3,512]{3,1,0,2:T(8,128)(2,1)S(1)}, bf16[2,128,3,512]{3,1,0,2:T(8,128)(2,1)}, u32[]{:S(2)}, u32[]{:S(2)}) %collective-permute-start.7) | collective-permute-done | bytes 786464 | tf_op jit(solution)/shard_map/ppermute | solution.py:29
  159.8 3.5 collective-permute-start.9
  163.3 3.9 %collective-permute-start.4 = (bf16[2,128,3,512]{3,1,0,2:T(8,128)(2,1)}, bf16[2,128,3,512]{3,1,0,2:T(8,128)(2,1)}, u32[]{:S(2)}, u32[]{:S(2)}) collective-permute-start(bf16[2,128,3,512]{3,1,0,2:T(8,128)(2,1)} %collective-permute-done.3), channel_id=1, source_target_pairs={{0,8},{8,0},{16,24},{24,16},{32,40},{40,32},{48,56},{56,48},{64,72... | collective-permute-start | bytes 2359304 | tf_op jit(solution)/shard_map/ppermute | solution.py:29
  168.6 8.3 %collective-permute-done.9 = bf16[2,128,3,512]{3,1,0,2:T(8,128)(2,1)} collective-permute-done((bf16[2,128,3,512]{3,1,0,2:T(8,128)(2,1)}, bf16[2,128,3,512]{3,1,0,2:T(8,128)(2,1)}, u32[]{:S(2)}, u32[]{:S(2)}) %collective-permute-start.9) | collective-permute-done | bytes 786464 | tf_op jit(solution)/shard_map/ppermute | solution.py:29
  176.9 4.5 %collective-permute-start.10 = (bf16[2,128,3,512]{3,1,0,2:T(8,128)(2,1)}, bf16[2,128,3,512]{3,1,0,2:T(8,128)(2,1)S(1)}, u32[]{:S(2)}, u32[]{:S(2)}) collective-permute-start(bf16[2,128,3,512]{3,1,0,2:T(8,128)(2,1)} %collective-permute-done.9), channel_id=1, source_target_pairs={{0,8},{8,0},{16,24},{24,16},{32,40},{40,32},{48,56},{56,48},{64,72... | collective-permute-start | bytes 2359304 | tf_op jit(solution)/shard_map/ppermute | solution.py:29
  181.4 3.0 copy_dynamic-update-slice_fusion.6
  184.3 3.3 collective-permute-done.13
  188.4 3.6 %copy_dynamic-update-slice_fusion.5 = bf16[8,2,2,128,3,512]{5,3,2,1,4,0:T(8,128)(2,1)} fusion(bf16[8,2,2,128,3,512]{5,3,2,1,4,0:T(8,128)(2,1)} %copy_dynamic-update-slice_fusion.6, bf16[1,2,1,128,3,512]{5,3,1,4,2,0:T(8,128)(2,1)} %bitcast.22, bf16[1,2,1,128,3,512]{5,3,1,4,2,0:T(8,128)(2,1)} %bitcast.21, pred[]{:T(512)S(6)} %eq.20), kind=kLoop, calls=%fused_computation.21 | loop fusion | flops 2359296 | bytes 3145729
  192.3 2.9 copy_dynamic-update-slice_fusion.4
  195.2 3.5 copy_dynamic-update-slice_fusion.3
  198.7 2.9 copy_dynamic-update-slice_fusion.2
  201.7 2.9 copy_dynamic-update-slice_fusion.1
  207.7 10.7 %rev.3 = bf16[8,2,2,128,3,512]{5,3,2,1,4,0:T(8,128)(2,1)} reverse(bf16[8,2,2,128,3,512]{5,3,2,1,4,0:T(8,128)(2,1)} %fusion.3), dimensions={0} | reverse | bytes 25165824 | tf_op jit(solution)/shard_map/rev | solution.py:73
  218.3 12.2 %fusion = bf16[8,2,2,128,3,512]{5,3,2,1,4,0:T(8,128)(2,1)} fusion(s32[]{:T(128)S(6)} %select_n.172, bf16[8,2,2,128,3,512]{5,3,2,1,4,0:T(8,128)(2,1)} %rev.3), kind=kLoop, calls=%fused_computation.2 | loop fusion | flops 6291456 | bytes 25165828 | tf_op jit(solution)/shard_map/concatenate | solution.py:74
  234.7 2.7 collective-permute-start.18
  243.7 3.3 select_bitcast_fusion
  247.0 74.3 %all-gather.7.cloned.1.call-done = bf16[4096,512]{1,0:T(8,128)(2,1)} async-done(((bf16[512,512]{1,0:T(8,128)(2,1)}), bf16[4096,512]{1,0:T(8,128)(2,1)}) %all-gather.7.cloned.1.call-update) | async-done | bytes 4194320 | tf_op jit(solution)/shard_map/all_gather | solution.py:138
  321.3 10.6 %convolution_bitcast_fusion = f32[512,3,512]{0,2,1:T(8,128)S(1)} fusion(bf16[8,512,512,1]{2,1,3,0:T(8,128)(2,1)} %bitcast.129, bf16[8,512,3,512]{3,1,2,0:T(8,128)(2,1)} %bitcast.108), kind=kOutput, calls=%fused_computation.6 | convolution fusion | flops 6442450944 | bytes 19922944 | tf_op jit(solution)/shard_map/ktf,kfin->tin/dot_general | solution.py:139
  336.4 6.5 %collective-permute-start.20 = (bf16[128,32,16]{0,2,1:T(8,128)(2,1)}, bf16[128,32,16]{0,2,1:T(8,128)(2,1)}, u32[]{:S(2)}, u32[]{:S(2)}) collective-permute-start(bf16[128,32,16]{0,2,1:T(8,128)(2,1)} %bitcast.44), channel_id=1, source_target_pairs={{0,8},{8,16},{16,24},{24,32},{32,40},{40,48},{48,56},{56,64},{64,7... | collective-permute-start | bytes 393224 | tf_op jit(solution)/shard_map/ppermute | solution.py:17
  343.0 3.3 fusion.19
  348.3 2.5 fusion.5
  (84 shorter events, 31.2 us)
Async XLA Ops:
  6.5 237.1 %copy-start = (bf16[32,128]{1,0:T(8,128)(2,1)S(1)}, bf16[32,128]{1,0:T(8,128)(2,1)}, u32[]{:S(2)}) copy-start(bf16[32,128]{1,0:T(8,128)(2,1)} %param.16) | copy-start | bytes 24580
  6.5 7.6 %copy-start.3 = (bf16[512,3,512]{2,0,1:T(8,128)(2,1)S(1)}, bf16[512,3,512]{2,0,1:T(8,128)(2,1)}, u32[]{:S(2)}) copy-start(bf16[512,3,512]{2,0,1:T(8,128)(2,1)} %param.9) | copy-start | bytes 4718596
  6.5 7.3 %copy-start.7 = (bf16[32,7]{0,1:T(8,128)(2,1)S(1)}, bf16[32,7]{0,1:T(8,128)(2,1)}, u32[]{:S(2)}) copy-start(bf16[32,7]{0,1:T(8,128)(2,1)} %param.11) | copy-start | bytes 1348
  6.5 69.5 %all-gather.5.cloned.1.call-start = ((), (), s32[]{:S(2)}) async-start(), calls=%async_computation.2 | async-start | bytes 4325376 | tf_op jit(solution)/shard_map/all_gather | solution.py:104
  7.3 7.0 %copy-start.8 = (bf16[512]{0:T(512)(128)(2,1)S(1)}, bf16[512]{0:T(512)(128)(2,1)}, u32[]{:S(2)}) copy-start(bf16[512]{0:T(512)(128)(2,1)} %param.12) | copy-start | bytes 3076
  7.3 223.3 %reduce-scatter.2.cloned.1.call-start = ((), (), s32[]{:S(2)}) async-start(), calls=%async_computation.1 | async-start | bytes 9437184 | tf_op jit(solution)/shard_map/reduce_scatter | solution.py:130
  8.7 6.0 %collective-permute-start = (bf16[6,512]{1,0:T(8,128)(2,1)S(1)}, bf16[6,512]{1,0:T(8,128)(2,1)S(1)}, u32[]{:S(2)}, u32[]{:S(2)}) collective-permute-start(bf16[6,512]{1,0:T(8,128)(2,1)S(1)} %slice_bitcast_fusion.1), channel_id=1, source_target_pairs={{0,8},{8,16},{16,24},{24,32},{32,40},{40,48},{48,56},{56,64},{64,7... | collective-permute-start | bytes 18440 | tf_op jit(solution)/shard_map/ppermute | solution.py:17
  93.6 227.7 %all-gather.7.cloned.1.call-start = ((), (), s32[]{:S(2)}) async-start(), calls=%async_computation.3 | async-start | bytes 4718592 | tf_op jit(solution)/shard_map/all_gather | solution.py:138
  94.5 10.4 %collective-permute-start.1 = (bf16[128,3,512]{2,0,1:T(8,128)(2,1)S(1)}, bf16[128,3,512]{2,0,1:T(8,128)(2,1)S(1)}, u32[]{:S(2)}, u32[]{:S(2)}) collective-permute-start(bf16[128,3,512]{2,0,1:T(8,128)(2,1)S(1)} %copy-done.6), channel_id=1, source_target_pairs={{0,16},{8,24},{16,0},{24,8},{32,48},{40,56},{48,32},{56,40},{64,80... | collective-permute-start | bytes 1179656 | tf_op jit(solution)/shard_map/ppermute | solution.py:29
  105.1 18.4 %collective-permute-start.3 = (bf16[2,128,3,512]{3,1,0,2:T(8,128)(2,1)S(1)}, bf16[2,128,3,512]{3,1,0,2:T(8,128)(2,1)}, u32[]{:S(2)}, u32[]{:S(2)}) collective-permute-start(bf16[2,128,3,512]{3,1,0,2:T(8,128)(2,1)S(1)} %get-tuple-element.12), channel_id=1, source_target_pairs={{0,32},{8,40},{16,48},{24,56},{32,64},{40,72},{48,80},{56,88},{64,... | collective-permute-start | bytes 2359304 | tf_op jit(solution)/shard_map/ppermute | solution.py:29
  123.5 18.7 %collective-permute-start.5 = (bf16[2,128,3,512]{3,1,0,2:T(8,128)(2,1)}, bf16[2,128,3,512]{3,1,0,2:T(8,128)(2,1)S(1)}, u32[]{:S(2)}, u32[]{:S(2)}) collective-permute-start(bf16[2,128,3,512]{3,1,0,2:T(8,128)(2,1)} %collective-permute-done.3), channel_id=1, source_target_pairs={{0,32},{8,40},{16,48},{24,56},{32,64},{40,72},{48,80},{56,88},{64,... | collective-permute-start | bytes 2359304 | tf_op jit(solution)/shard_map/ppermute | solution.py:29
  127.0 18.6 %collective-permute-start.11 = (bf16[2,128,3,512]{3,1,0,2:T(8,128)(2,1)S(1)}, bf16[2,128,3,512]{3,1,0,2:T(8,128)(2,1)S(1)}, u32[]{:S(2)}, u32[]{:S(2)}) collective-permute-start(bf16[2,128,3,512]{3,1,0,2:T(8,128)(2,1)S(1)} %get-tuple-element.12), channel_id=1, source_target_pairs={{0,224},{8,232},{16,240},{24,248},{32,0},{40,8},{48,16},{56,24},{6... | collective-permute-start | bytes 2359304 | tf_op jit(solution)/shard_map/ppermute | solution.py:29
  142.2 17.6 %collective-permute-start.7 = (bf16[2,128,3,512]{3,1,0,2:T(8,128)(2,1)S(1)}, bf16[2,128,3,512]{3,1,0,2:T(8,128)(2,1)}, u32[]{:S(2)}, u32[]{:S(2)}) collective-permute-start(bf16[2,128,3,512]{3,1,0,2:T(8,128)(2,1)S(1)} %collective-permute-done.5), channel_id=1, source_target_pairs={{0,32},{8,40},{16,48},{24,56},{32,64},{40,72},{48,80},{56,88},{64,... | collective-permute-start | bytes 2359304 | tf_op jit(solution)/shard_map/ppermute | solution.py:29
  145.6 21.6 %collective-permute-start.12 = (bf16[2,128,3,512]{3,1,0,2:T(8,128)(2,1)S(1)}, bf16[2,128,3,512]{3,1,0,2:T(8,128)(2,1)S(1)}, u32[]{:S(2)}, u32[]{:S(2)}) collective-permute-start(bf16[2,128,3,512]{3,1,0,2:T(8,128)(2,1)S(1)} %collective-permute-done.11), channel_id=1, source_target_pairs={{0,224},{8,232},{16,240},{24,248},{32,0},{40,8},{48,16},{56,24},{6... | collective-permute-start | bytes 2359304 | tf_op jit(solution)/shard_map/ppermute | solution.py:29
  145.6 21.8 %collective-permute-start.2 = (bf16[2,128,3,512]{3,1,0,2:T(8,128)(2,1)S(1)}, bf16[2,128,3,512]{3,1,0,2:T(8,128)(2,1)S(1)}, u32[]{:S(2)}, u32[]{:S(2)}) collective-permute-start(bf16[2,128,3,512]{3,1,0,2:T(8,128)(2,1)S(1)} %get-tuple-element.12), channel_id=1, source_target_pairs={{0,8},{8,0},{16,24},{24,16},{32,40},{40,32},{48,56},{56,48},{64,72... | collective-permute-start | bytes 2359304 | tf_op jit(solution)/shard_map/ppermute | solution.py:29
  159.8 17.1 %collective-permute-start.9 = (bf16[2,128,3,512]{3,1,0,2:T(8,128)(2,1)}, bf16[2,128,3,512]{3,1,0,2:T(8,128)(2,1)}, u32[]{:S(2)}, u32[]{:S(2)}) collective-permute-start(bf16[2,128,3,512]{3,1,0,2:T(8,128)(2,1)} %collective-permute-done.7), channel_id=1, source_target_pairs={{0,32},{8,40},{16,48},{24,56},{32,64},{40,72},{48,80},{56,88},{64,... | collective-permute-start | bytes 2359304 | tf_op jit(solution)/shard_map/ppermute | solution.py:29
  163.3 21.0 %collective-permute-start.4 = (bf16[2,128,3,512]{3,1,0,2:T(8,128)(2,1)}, bf16[2,128,3,512]{3,1,0,2:T(8,128)(2,1)}, u32[]{:S(2)}, u32[]{:S(2)}) collective-permute-start(bf16[2,128,3,512]{3,1,0,2:T(8,128)(2,1)} %collective-permute-done.3), channel_id=1, source_target_pairs={{0,8},{8,0},{16,24},{24,16},{32,40},{40,32},{48,56},{56,48},{64,72... | collective-permute-start | bytes 2359304 | tf_op jit(solution)/shard_map/ppermute | solution.py:29
  167.2 20.4 %collective-permute-start.13 = (bf16[2,128,3,512]{3,1,0,2:T(8,128)(2,1)S(1)}, bf16[2,128,3,512]{3,1,0,2:T(8,128)(2,1)}, u32[]{:S(2)}, u32[]{:S(2)}) collective-permute-start(bf16[2,128,3,512]{3,1,0,2:T(8,128)(2,1)S(1)} %collective-permute-done.12), channel_id=1, source_target_pairs={{0,224},{8,232},{16,240},{24,248},{32,0},{40,8},{48,16},{56,24},{6... | collective-permute-start | bytes 2359304 | tf_op jit(solution)/shard_map/ppermute | solution.py:29
  167.2 24.9 %collective-permute-start.6 = (bf16[2,128,3,512]{3,1,0,2:T(8,128)(2,1)S(1)}, bf16[2,128,3,512]{3,1,0,2:T(8,128)(2,1)}, u32[]{:S(2)}, u32[]{:S(2)}) collective-permute-start(bf16[2,128,3,512]{3,1,0,2:T(8,128)(2,1)S(1)} %collective-permute-done.5), channel_id=1, source_target_pairs={{0,8},{8,0},{16,24},{24,16},{32,40},{40,32},{48,56},{56,48},{64,72... | collective-permute-start | bytes 2359304 | tf_op jit(solution)/shard_map/ppermute | solution.py:29
  168.3 26.9 %collective-permute-start.8 = (bf16[2,128,3,512]{3,1,0,2:T(8,128)(2,1)}, bf16[2,128,3,512]{3,1,0,2:T(8,128)(2,1)}, u32[]{:S(2)}, u32[]{:S(2)}) collective-permute-start(bf16[2,128,3,512]{3,1,0,2:T(8,128)(2,1)} %collective-permute-done.7), channel_id=1, source_target_pairs={{0,8},{8,0},{16,24},{24,16},{32,40},{40,32},{48,56},{56,48},{64,72... | collective-permute-start | bytes 2359304 | tf_op jit(solution)/shard_map/ppermute | solution.py:29
  176.9 21.9 %collective-permute-start.10 = (bf16[2,128,3,512]{3,1,0,2:T(8,128)(2,1)}, bf16[2,128,3,512]{3,1,0,2:T(8,128)(2,1)S(1)}, u32[]{:S(2)}, u32[]{:S(2)}) collective-permute-start(bf16[2,128,3,512]{3,1,0,2:T(8,128)(2,1)} %collective-permute-done.9), channel_id=1, source_target_pairs={{0,8},{8,0},{16,24},{24,16},{32,40},{40,32},{48,56},{56,48},{64,72... | collective-permute-start | bytes 2359304 | tf_op jit(solution)/shard_map/ppermute | solution.py:29
  184.3 21.8 %collective-permute-start.16 = (bf16[2,128,3,512]{3,1,0,2:T(8,128)(2,1)S(1)}, bf16[2,128,3,512]{3,1,0,2:T(8,128)(2,1)S(1)}, u32[]{:S(2)}, u32[]{:S(2)}) collective-permute-start(bf16[2,128,3,512]{3,1,0,2:T(8,128)(2,1)S(1)} %collective-permute-done.11), channel_id=1, source_target_pairs={{0,8},{8,0},{16,24},{24,16},{32,40},{40,32},{48,56},{56,48},{64,72... | collective-permute-start | bytes 2359304 | tf_op jit(solution)/shard_map/ppermute | solution.py:29
  187.6 14.1 %collective-permute-start.14 = (bf16[2,128,3,512]{3,1,0,2:T(8,128)(2,1)}, bf16[2,128,3,512]{3,1,0,2:T(8,128)(2,1)S(1)}, u32[]{:S(2)}, u32[]{:S(2)}) collective-permute-start(bf16[2,128,3,512]{3,1,0,2:T(8,128)(2,1)} %collective-permute-done.13), channel_id=1, source_target_pairs={{0,8},{8,0},{16,24},{24,16},{32,40},{40,32},{48,56},{56,48},{64,72... | collective-permute-start | bytes 2359304 | tf_op jit(solution)/shard_map/ppermute | solution.py:29
  192.1 12.6 %collective-permute-start.15 = (bf16[2,128,3,512]{3,1,0,2:T(8,128)(2,1)S(1)}, bf16[2,128,3,512]{3,1,0,2:T(8,128)(2,1)S(1)}, u32[]{:S(2)}, u32[]{:S(2)}) collective-permute-start(bf16[2,128,3,512]{3,1,0,2:T(8,128)(2,1)S(1)} %collective-permute-done.12), channel_id=1, source_target_pairs={{0,8},{8,0},{16,24},{24,16},{32,40},{40,32},{48,56},{56,48},{64,72... | collective-permute-start | bytes 2359304 | tf_op jit(solution)/shard_map/ppermute | solution.py:29
  218.3 12.3 %copy-start.4 = (bf16[512,512]{1,0:T(8,128)(2,1)S(1)}, bf16[512,512]{1,0:T(8,128)(2,1)}, u32[]{:S(2)}) copy-start(bf16[512,512]{1,0:T(8,128)(2,1)} %param.10) | copy-start | bytes 1572868
  230.6 12.0 %copy-start.2 = (f32[1,512,512]{2,1,0:T(8,128)S(1)}, f32[1,512,512]{2,1,0:T(8,128)}, u32[]{:S(2)}) copy-start(f32[1,512,512]{2,1,0:T(8,128)} %reduce-scatter.2.cloned.1.call-done) | copy-start | bytes 3145732
  232.1 11.4 %copy-start.9 = (bf16[512]{0:T(512)(128)(2,1)S(1)}, bf16[512]{0:T(512)(128)(2,1)}, u32[]{:S(2)}) copy-start(bf16[512]{0:T(512)(128)(2,1)} %param.17) | copy-start | bytes 3076
  232.1 2.5 collective-permute-start.17
  234.7 3.9 %collective-permute-start.18 = (f32[512]{0:T(512)S(1)}, f32[512]{0:T(512)S(1)}, u32[]{:S(2)}, u32[]{:S(2)}) collective-permute-start(f32[512]{0:T(512)S(1)} %add.90), channel_id=1, source_target_pairs={{0,2},{1,3},{2,0},{3,1},{4,6},{5,7},{6,4},{7,5},{8,10},{9,11},{10,... | collective-permute-start | bytes 6152 | tf_op jit(solution)/shard_map/ppermute | solution.py:83
  238.6 3.9 %collective-permute-start.19 = (f32[512]{0:T(512)S(1)}, f32[512]{0:T(512)S(1)}, u32[]{:S(2)}, u32[]{:S(2)}) collective-permute-start(f32[512]{0:T(512)S(1)} %add.91), channel_id=1, source_target_pairs={{0,4},{1,5},{2,6},{3,7},{4,0},{5,1},{6,2},{7,3},{8,12},{9,13},{10,... | collective-permute-start | bytes 6152 | tf_op jit(solution)/shard_map/ppermute | solution.py:83
  336.4 11.8 %collective-permute-start.20 = (bf16[128,32,16]{0,2,1:T(8,128)(2,1)}, bf16[128,32,16]{0,2,1:T(8,128)(2,1)}, u32[]{:S(2)}, u32[]{:S(2)}) collective-permute-start(bf16[128,32,16]{0,2,1:T(8,128)(2,1)} %bitcast.44), channel_id=1, source_target_pairs={{0,8},{8,16},{16,24},{24,32},{32,40},{40,48},{48,56},{56,64},{64,7... | collective-permute-start | bytes 393224 | tf_op jit(solution)/shard_map/ppermute | solution.py:17
  343.0 3.3 slice-start
  (3 other events, 5.0 us)
Sparse Core Ops, SparseCore 0:
  9.2 66.7 all-gather.4
  93.7 119.4 reduce-scatter.1
  243.7 77.5 all-gather.6

commit v3 on v2

--- a/solution.py
+++ b/solution.py
@@ -61,18 +61,17 @@
     me = lax.axis_index("seq")
     my_z = me // 4
     mine_first = me % 2 == 0
-    by_offset = jnp.stack(
-        [
-            jnp.where(
-                mine_first, jnp.stack([mine, partner], axis=1), jnp.stack([partner, mine], axis=1)
-            )
-            for _, mine, partner in sorted(pieces)
-        ]
-    )
-    z_size = by_offset.shape[0]
-    reverse = by_offset[::-1]
-    doubled = jnp.concatenate([reverse, reverse], axis=0)
-    return lax.dynamic_slice_in_dim(doubled, (z_size - 1 - my_z) % z_size, z_size, axis=0)
+    z_size = len(pieces)
+    full = None
+    for k, mine, partner in sorted(pieces):
+        block = jnp.where(
+            mine_first, jnp.stack([mine, partner], axis=1), jnp.stack([partner, mine], axis=1)
+        )
+        if full is None:
+            full = jnp.zeros((z_size,) + block.shape, block.dtype)
+        start = ((my_z - k) % z_size,) + (0,) * block.ndim
+        full = lax.dynamic_update_slice(full, block[None], start)
+    return full
 
 
 def tp_sum(value):
@@ -103,8 +102,8 @@
     tp_size = lax.axis_size("tp")
     stacked = lax.all_gather(w_out, "seq", axis=0, tiled=False)
     per_tp = stacked.reshape(tp_size, stacked.shape[0] // tp_size, *stacked.shape[1:])
-    partial = jnp.einsum("tc,kjcf->ktjf", y_se, per_tp, preferred_element_type=jnp.float32)
-    return partial.reshape(tp_size, y_se.shape[0], -1)
+    partial = jnp.einsum("tc,kjcf->tkjf", y_se, per_tp, preferred_element_type=jnp.float32)
+    return partial.reshape(y_se.shape[0], tp_size, -1)
 
 
 def per_device(qkv_se, residual, taps_se, skip_se, w_out, norm_gain, w_in, taps_mr, skip_mr):
@@ -127,7 +126,7 @@
     )
     gain_full = norm_gain.astype(jnp.float32)
     partial_out = project_out(y_se, w_out)
-    share = lax.psum_scatter(partial_out, "tp", scatter_dimension=0, tiled=True)[0]
+    share = lax.psum_scatter(partial_out, "tp", scatter_dimension=1, tiled=True)[:, 0]
     w_full = absolute_rows(gather_rows(w_in))
     share, w_full = lax.optimization_barrier((share, w_full))
     stream = residual.astype(jnp.float32) + share

time: 362 us -> 380 us (1.050)
  local copies, waits for them, and re-layouts: 29.8 us -> 76.2 us
  waiting for transfers between devices: 204 us -> 183 us
  other arithmetic: 41.3 us -> 32.4 us
    dynamic_update_slice x0 -> x2, local copies, waits for them, and re-layouts: none -> 33.4 us  [absolute_rows(): full = lax.dynamic_update_slice(full, block[None], start)]
    dynamic_update_slice x0 -> x7, other arithmetic: none -> 20.8 us  [absolute_rows(): full = lax.dynamic_update_slice(full, block[None], start)]
    unnamed x7 -> x0, other arithmetic: 20.4 us -> none
    reshape x1 -> x2, local copies, waits for them, and re-layouts: 9.12 us -> 25.6 us  [the longest x1 19.1 us: per_device(): w_full.reshape(gathered.shape[0], gathered.shape[2], *w_in.shape[1:])]
    all_gather x1, waiting for transfers between devices: 74.3 us -> 58.5 us  [per_device(): gathered = lax.all_gather(normed, 'tp', axis=0, tiled=False)]
    concatenate x1 -> x0, other arithmetic: 12.2 us -> none  [absolute_rows(): doubled = jnp.concatenate([reverse, reverse], axis=0)]
    rev x1 -> x0, local copies, waits for them, and re-layouts: 10.7 us -> none  [absolute_rows(): reverse = by_offset[::-1]]
    broadcast_in_dim x0 -> x1, local copies, waits for them, and re-layouts: none -> 6.09 us  [absolute_rows(): full = jnp.zeros((z_size,) + block.shape, block.dtype)]
  transfers between devices with their start and end apart: 24 -> 24, of which waited for: 12 -> 10; matrix products, arithmetic and copies ran while one was open for 16% -> 25% of each run, Pallas kernels for 0% -> 0%
where the time goes in v3:
time: 380 us; the launch traced here: 378 us
  waiting for transfers between devices  183 us (48%)
  local copies, waits for them, and re-layouts  76.2 us (20%)
  starting transfers between devices  44.3 us (12%)
  other arithmetic  32.4 us (9%)
  matrix products  28.3 us (7%)
  between operations  13.3 us (4%)
    ppermute x16, waiting for transfers between devices, exchange(): return lax.ppermute(block, axis, pairs)  59.9 us
    all_gather x1, waiting for transfers between devices, project_out(): stacked = lax.all_gather(w_out, 'seq', axis=0, tiled=False)  59.7 us
    all_gather x1, waiting for transfers between devices, per_device(): gathered = lax.all_gather(normed, 'tp', axis=0, tiled=False)  58.5 us
    dynamic_update_slice x2, local copies, waits for them, and re-layouts, absolute_rows(): full = lax.dynamic_update_slice(full, block[None], start)  33.4 us
    ppermute x16, starting transfers between devices, exchange(): return lax.ppermute(block, axis, pairs)  27 us
    dynamic_update_slice x7, other arithmetic, absolute_rows(): full = lax.dynamic_update_slice(full, block[None], start)  20.8 us
    reshape x1, local copies, waits for them, and re-layouts, per_device(): w_full.reshape(gathered.shape[0], gathered.shape[2], *w_in.shape[1:])  19.1 us
    ppermute x2, starting transfers between devices, shifted(): return lax.ppermute(block, axis, route)  11.7 us
  transfers between devices with their start and end apart: 24, of which 10 were waited for; matrix products, arithmetic and copies ran while one was open for 25% of the time, Pallas kernels for 0%

profile of v3, /device:TPU:105, one launch (start us, length us, event | category | flops | bytes accessed | tf_op | source)
XLA Modules:
  0.0 377.5 jit_solution(2928596413458119773)
XLA Ops:
  8.7 5.2 %collective-permute-start = (bf16[6,512]{1,0:T(8,128)(2,1)S(1)}, bf16[6,512]{1,0:T(8,128)(2,1)S(1)}, u32[]{:S(2)}, u32[]{:S(2)}) collective-permute-start(bf16[6,512]{1,0:T(8,128)(2,1)S(1)} %slice_bitcast_fusion.1), channel_id=1, source_target_pairs={{0,8},{8,16},{16,24},{24,32},{32,40},{40,48},{48,56},{56,64},{64,7... | collective-permute-start | bytes 18440 | tf_op jit(solution)/shard_map/ppermute | solution.py:17
  16.3 59.7 %all-gather.5.cloned.1.call-done = bf16[16384,128]{1,0:T(8,128)(2,1)} async-done(((bf16[512,128]{1,0:T(8,128)(2,1)}), bf16[16384,128]{1,0:T(8,128)(2,1)}) %all-gather.5.cloned.1.call-update) | async-done | bytes 4194320 | tf_op jit(solution)/shard_map/all_gather | solution.py:103
  76.0 6.4 %copy.29 = bf16[8,4,512,128]{2,3,1,0:T(8,128)(2,1)} copy(bf16[8,4,512,128]{3,2,1,0:T(8,128)(2,1)} %bitcast.101) | data formatting | bytes 8388608 | tf_op jit(solution)/shard_map/reshape | solution.py:104
  82.5 8.7 %fusion.29 = f32[512,8,512]{2,0,1:T(8,128)} fusion(bf16[8,512,512]{2,1,0:T(8,128)(2,1)} %bitcast.102, f32[518,512]{1,0:T(8,128)S(1)} %maximum_convert_fusion, f32[512]{0:T(512)S(1)} %convert_element_type.78, f32[512]{0:T(512)S(1)} %bitcast.110, f32[512]{0:T(512)S(1)} %bitcast.111, f32[512]{0:T(512)S(1)} %bitcast.112, f32[512]{0:T(512)S(1)} %bitcast.113, ...), kind=kOutput, calls=%fused_computation.59 | convolution fusion | flops 2152464384 | bytes 20987904 | tf_op jit(solution)/shard_map/tc,kjcf->tkjf/dot_general | solution.py:105
  93.4 9.1 %collective-permute-done.1 = bf16[128,3,512]{2,0,1:T(8,128)(2,1)S(1)} collective-permute-done((bf16[128,3,512]{2,0,1:T(8,128)(2,1)S(1)}, bf16[128,3,512]{2,0,1:T(8,128)(2,1)S(1)}, u32[]{:S(2)}, u32[]{:S(2)}) %collective-permute-start.1) | collective-permute-done | bytes 393248 | tf_op jit(solution)/shard_map/ppermute | solution.py:29
  102.7 2.6 collective-permute-start.3
  105.4 15.8 %collective-permute-done.3 = bf16[2,128,3,512]{3,1,2,0:T(8,128)(2,1)S(1)} collective-permute-done((bf16[2,128,3,512]{3,1,2,0:T(8,128)(2,1)S(1)}, bf16[2,128,3,512]{3,1,2,0:T(8,128)(2,1)S(1)}, u32[]{:S(2)}, u32[]{:S(2)}) %collective-permute-start.3) | collective-permute-done | bytes 786464 | tf_op jit(solution)/shard_map/ppermute | solution.py:29
  121.1 3.4 collective-permute-start.5
  124.5 14.9 %collective-permute-done.5 = bf16[2,128,3,512]{3,1,2,0:T(8,128)(2,1)} collective-permute-done((bf16[2,128,3,512]{3,1,2,0:T(8,128)(2,1)S(1)}, bf16[2,128,3,512]{3,1,2,0:T(8,128)(2,1)}, u32[]{:S(2)}, u32[]{:S(2)}) %collective-permute-start.5) | collective-permute-done | bytes 786464 | tf_op jit(solution)/shard_map/ppermute | solution.py:29
  139.4 3.5 collective-permute-start.7
  142.9 3.1 collective-permute-start.2
  146.2 11.1 %collective-permute-done.7 = bf16[2,128,3,512]{3,1,2,0:T(8,128)(2,1)} collective-permute-done((bf16[2,128,3,512]{3,1,2,0:T(8,128)(2,1)}, bf16[2,128,3,512]{3,1,2,0:T(8,128)(2,1)}, u32[]{:S(2)}, u32[]{:S(2)}) %collective-permute-start.7) | collective-permute-done | bytes 786464 | tf_op jit(solution)/shard_map/ppermute | solution.py:29
  157.3 3.4 collective-permute-start.9
  160.7 4.0 %collective-permute-start.16 = (bf16[2,128,3,512]{3,1,2,0:T(8,128)(2,1)}, bf16[2,128,3,512]{3,1,2,0:T(8,128)(2,1)}, u32[]{:S(2)}, u32[]{:S(2)}) collective-permute-start(bf16[2,128,3,512]{3,1,2,0:T(8,128)(2,1)} %collective-permute-done.11), channel_id=1, source_target_pairs={{0,8},{8,0},{16,24},{24,16},{32,40},{40,32},{48,56},{56,48},{64,72... | collective-permute-start | bytes 2359304 | tf_op jit(solution)/shard_map/ppermute | solution.py:29
  165.2 9.0 %collective-permute-done.9 = bf16[2,128,3,512]{3,1,2,0:T(8,128)(2,1)} collective-permute-done((bf16[2,128,3,512]{3,1,2,0:T(8,128)(2,1)}, bf16[2,128,3,512]{3,1,2,0:T(8,128)(2,1)}, u32[]{:S(2)}, u32[]{:S(2)}) %collective-permute-start.9) | collective-permute-done | bytes 786464 | tf_op jit(solution)/shard_map/ppermute | solution.py:29
  174.2 4.6 %collective-permute-start.10 = (bf16[2,128,3,512]{3,1,2,0:T(8,128)(2,1)}, bf16[2,128,3,512]{3,1,2,0:T(8,128)(2,1)}, u32[]{:S(2)}, u32[]{:S(2)}) collective-permute-start(bf16[2,128,3,512]{3,1,2,0:T(8,128)(2,1)} %collective-permute-done.9), channel_id=1, source_target_pairs={{0,8},{8,0},{16,24},{24,16},{32,40},{40,32},{48,56},{56,48},{64,72... | collective-permute-start | bytes 2359304 | tf_op jit(solution)/shard_map/ppermute | solution.py:29
  178.8 6.1 %broadcast_in_dim.17 = bf16[8,2,2,128,3,512]{5,3,4,1,2,0:T(8,128)(2,1)} broadcast(bf16[]{:T(256)} %constant.109.clone.1), dimensions={} | broadcast | bytes 12582914 | tf_op jit(solution)/shard_map/broadcast_in_dim | solution.py:71
  191.7 3.6 fusion.4
  195.3 3.5 fusion.5
  198.8 3.6 fusion.6
  202.4 3.6 fusion.7
  206.0 3.6 fusion.8
  209.5 31.2 %copy.30 = bf16[8,2,2,128,3,512]{3,2,1,5,0,4:T(2,128)(2,1)} copy(bf16[8,2,2,128,3,512]{5,3,4,1,2,0:T(8,128)(2,1)} %fusion.8) | data formatting | bytes 25165824 | tf_op jit(solution)/shard_map/dynamic_update_slice | solution.py:73
  240.7 2.3 constant_dynamic-update-slice_fusion
  246.9 2.7 collective-permute-start.18
  257.2 3.3 select_bitcast_fusion
  260.4 19.1 %reshape.552 = bf16[8,512,3,512]{1,3,0,2:T(8,128)(2,1)} reshape(bf16[8,2,2,128,3,512]{3,2,1,5,0,4:T(2,128)(2,1)} %constant_dynamic-update-slice_fusion) | data formatting | bytes 25165824 | tf_op jit(solution)/shard_map/reshape | solution.py:141
  279.6 58.5 %all-gather.7.cloned.1.call-done = bf16[4096,512]{1,0:T(8,128)(2,1)} async-done(((bf16[512,512]{1,0:T(8,128)(2,1)}), bf16[4096,512]{1,0:T(8,128)(2,1)}) %all-gather.7.cloned.1.call-update) | async-done | bytes 4194320 | tf_op jit(solution)/shard_map/all_gather | solution.py:137
  338.1 10.6 %convolution_bitcast_fusion = f32[512,3,512]{0,2,1:T(8,128)S(1)} fusion(bf16[8,512,512,1]{2,1,0,3:T(8,128)(2,1)} %bitcast.116, bf16[8,512,3,512]{1,3,0,2:T(8,128)(2,1)} %reshape.552), kind=kOutput, calls=%fused_computation.3 | convolution fusion | flops 6442450944 | bytes 19922944 | tf_op jit(solution)/shard_map/ktf,kfin->tin/dot_general | solution.py:138
  353.2 6.5 %collective-permute-start.20 = (bf16[128,32,16]{0,2,1:T(8,128)(2,1)}, bf16[128,32,16]{0,2,1:T(8,128)(2,1)}, u32[]{:S(2)}, u32[]{:S(2)}) collective-permute-start(bf16[128,32,16]{0,2,1:T(8,128)(2,1)} %bitcast.41), channel_id=1, source_target_pairs={{0,8},{8,16},{16,24},{24,32},{32,40},{40,48},{48,56},{56,64},{64,7... | collective-permute-start | bytes 393224 | tf_op jit(solution)/shard_map/ppermute | solution.py:17
  359.7 3.2 fusion.24
  365.0 2.5 fusion.10
  (77 shorter events, 35.8 us)
Async XLA Ops:
  6.5 250.6 %copy-start = (bf16[32,128]{1,0:T(8,128)(2,1)S(1)}, bf16[32,128]{1,0:T(8,128)(2,1)}, u32[]{:S(2)}) copy-start(bf16[32,128]{1,0:T(8,128)(2,1)} %param.16) | copy-start | bytes 24580
  6.5 9.6 %copy-start.3 = (bf16[512]{0:T(512)(128)(2,1)S(1)}, bf16[512]{0:T(512)(128)(2,1)}, u32[]{:S(2)}) copy-start(bf16[512]{0:T(512)(128)(2,1)} %param.12) | copy-start | bytes 3076
  6.5 69.5 %all-gather.5.cloned.1.call-start = ((), (), s32[]{:S(2)}) async-start(), calls=%async_computation.2 | async-start | bytes 4325376 | tf_op jit(solution)/shard_map/all_gather | solution.py:103
  7.3 235.7 %reduce-scatter.2.cloned.1.call-start = ((), (), s32[]{:S(2)}) async-start(), calls=%async_computation.1 | async-start | bytes 9437184 | tf_op jit(solution)/shard_map/reduce_scatter | solution.py:129
  8.7 7.5 %collective-permute-start = (bf16[6,512]{1,0:T(8,128)(2,1)S(1)}, bf16[6,512]{1,0:T(8,128)(2,1)S(1)}, u32[]{:S(2)}, u32[]{:S(2)}) collective-permute-start(bf16[6,512]{1,0:T(8,128)(2,1)S(1)} %slice_bitcast_fusion.1), channel_id=1, source_target_pairs={{0,8},{8,16},{16,24},{24,32},{32,40},{40,48},{48,56},{56,64},{64,7... | collective-permute-start | bytes 18440 | tf_op jit(solution)/shard_map/ppermute | solution.py:17
  91.2 1.0 copy-start.2
  91.2 246.9 %all-gather.7.cloned.1.call-start = ((), (), s32[]{:S(2)}) async-start(), calls=%async_computation.3 | async-start | bytes 4718592 | tf_op jit(solution)/shard_map/all_gather | solution.py:137
  92.2 10.4 %collective-permute-start.1 = (bf16[128,3,512]{2,0,1:T(8,128)(2,1)S(1)}, bf16[128,3,512]{2,0,1:T(8,128)(2,1)S(1)}, u32[]{:S(2)}, u32[]{:S(2)}) collective-permute-start(bf16[128,3,512]{2,0,1:T(8,128)(2,1)S(1)} %copy-done.2), channel_id=1, source_target_pairs={{0,16},{8,24},{16,0},{24,8},{32,48},{40,56},{48,32},{56,40},{64,80... | collective-permute-start | bytes 1179656 | tf_op jit(solution)/shard_map/ppermute | solution.py:29
  102.7 18.4 %collective-permute-start.3 = (bf16[2,128,3,512]{3,1,2,0:T(8,128)(2,1)S(1)}, bf16[2,128,3,512]{3,1,2,0:T(8,128)(2,1)S(1)}, u32[]{:S(2)}, u32[]{:S(2)}) collective-permute-start(bf16[2,128,3,512]{3,1,2,0:T(8,128)(2,1)S(1)} %get-tuple-element.12), channel_id=1, source_target_pairs={{0,32},{8,40},{16,48},{24,56},{32,64},{40,72},{48,80},{56,88},{64,... | collective-permute-start | bytes 2359304 | tf_op jit(solution)/shard_map/ppermute | solution.py:29
  121.1 18.3 %collective-permute-start.5 = (bf16[2,128,3,512]{3,1,2,0:T(8,128)(2,1)S(1)}, bf16[2,128,3,512]{3,1,2,0:T(8,128)(2,1)}, u32[]{:S(2)}, u32[]{:S(2)}) collective-permute-start(bf16[2,128,3,512]{3,1,2,0:T(8,128)(2,1)S(1)} %collective-permute-done.3), channel_id=1, source_target_pairs={{0,32},{8,40},{16,48},{24,56},{32,64},{40,72},{48,80},{56,88},{64,... | collective-permute-start | bytes 2359304 | tf_op jit(solution)/shard_map/ppermute | solution.py:29
  124.5 18.4 %collective-permute-start.11 = (bf16[2,128,3,512]{3,1,2,0:T(8,128)(2,1)S(1)}, bf16[2,128,3,512]{3,1,2,0:T(8,128)(2,1)}, u32[]{:S(2)}, u32[]{:S(2)}) collective-permute-start(bf16[2,128,3,512]{3,1,2,0:T(8,128)(2,1)S(1)} %get-tuple-element.12), channel_id=1, source_target_pairs={{0,224},{8,232},{16,240},{24,248},{32,0},{40,8},{48,16},{56,24},{6... | collective-permute-start | bytes 2359304 | tf_op jit(solution)/shard_map/ppermute | solution.py:29
  139.4 17.9 %collective-permute-start.7 = (bf16[2,128,3,512]{3,1,2,0:T(8,128)(2,1)}, bf16[2,128,3,512]{3,1,2,0:T(8,128)(2,1)}, u32[]{:S(2)}, u32[]{:S(2)}) collective-permute-start(bf16[2,128,3,512]{3,1,2,0:T(8,128)(2,1)} %collective-permute-done.5), channel_id=1, source_target_pairs={{0,32},{8,40},{16,48},{24,56},{32,64},{40,72},{48,80},{56,88},{64,... | collective-permute-start | bytes 2359304 | tf_op jit(solution)/shard_map/ppermute | solution.py:29
  142.9 17.8 %collective-permute-start.12 = (bf16[2,128,3,512]{3,1,2,0:T(8,128)(2,1)}, bf16[2,128,3,512]{3,1,2,0:T(8,128)(2,1)}, u32[]{:S(2)}, u32[]{:S(2)}) collective-permute-start(bf16[2,128,3,512]{3,1,2,0:T(8,128)(2,1)} %collective-permute-done.11), channel_id=1, source_target_pairs={{0,224},{8,232},{16,240},{24,248},{32,0},{40,8},{48,16},{56,24},{6... | collective-permute-start | bytes 2359304 | tf_op jit(solution)/shard_map/ppermute | solution.py:29
  142.9 21.8 %collective-permute-start.2 = (bf16[2,128,3,512]{3,1,2,0:T(8,128)(2,1)S(1)}, bf16[2,128,3,512]{3,1,2,0:T(8,128)(2,1)S(1)}, u32[]{:S(2)}, u32[]{:S(2)}) collective-permute-start(bf16[2,128,3,512]{3,1,2,0:T(8,128)(2,1)S(1)} %get-tuple-element.12), channel_id=1, source_target_pairs={{0,8},{8,0},{16,24},{24,16},{32,40},{40,32},{48,56},{56,48},{64,72... | collective-permute-start | bytes 2359304 | tf_op jit(solution)/shard_map/ppermute | solution.py:29
  146.1 18.7 %collective-permute-start.4 = (bf16[2,128,3,512]{3,1,2,0:T(8,128)(2,1)S(1)}, bf16[2,128,3,512]{3,1,2,0:T(8,128)(2,1)S(1)}, u32[]{:S(2)}, u32[]{:S(2)}) collective-permute-start(bf16[2,128,3,512]{3,1,2,0:T(8,128)(2,1)S(1)} %collective-permute-done.3), channel_id=1, source_target_pairs={{0,8},{8,0},{16,24},{24,16},{32,40},{40,32},{48,56},{56,48},{64,72... | collective-permute-start | bytes 2359304 | tf_op jit(solution)/shard_map/ppermute | solution.py:29
  157.3 16.9 %collective-permute-start.9 = (bf16[2,128,3,512]{3,1,2,0:T(8,128)(2,1)}, bf16[2,128,3,512]{3,1,2,0:T(8,128)(2,1)}, u32[]{:S(2)}, u32[]{:S(2)}) collective-permute-start(bf16[2,128,3,512]{3,1,2,0:T(8,128)(2,1)} %collective-permute-done.7), channel_id=1, source_target_pairs={{0,32},{8,40},{16,48},{24,56},{32,64},{40,72},{48,80},{56,88},{64,... | collective-permute-start | bytes 2359304 | tf_op jit(solution)/shard_map/ppermute | solution.py:29
  160.7 25.7 %collective-permute-start.13 = (bf16[2,128,3,512]{3,1,2,0:T(8,128)(2,1)}, bf16[2,128,3,512]{3,1,2,0:T(8,128)(2,1)}, u32[]{:S(2)}, u32[]{:S(2)}) collective-permute-start(bf16[2,128,3,512]{3,1,2,0:T(8,128)(2,1)} %collective-permute-done.12), channel_id=1, source_target_pairs={{0,224},{8,232},{16,240},{24,248},{32,0},{40,8},{48,16},{56,24},{6... | collective-permute-start | bytes 2359304 | tf_op jit(solution)/shard_map/ppermute | solution.py:29
  160.7 27.1 %collective-permute-start.16 = (bf16[2,128,3,512]{3,1,2,0:T(8,128)(2,1)}, bf16[2,128,3,512]{3,1,2,0:T(8,128)(2,1)}, u32[]{:S(2)}, u32[]{:S(2)}) collective-permute-start(bf16[2,128,3,512]{3,1,2,0:T(8,128)(2,1)} %collective-permute-done.11), channel_id=1, source_target_pairs={{0,8},{8,0},{16,24},{24,16},{32,40},{40,32},{48,56},{56,48},{64,72... | collective-permute-start | bytes 2359304 | tf_op jit(solution)/shard_map/ppermute | solution.py:29
  164.7 27.0 %collective-permute-start.6 = (bf16[2,128,3,512]{3,1,2,0:T(8,128)(2,1)}, bf16[2,128,3,512]{3,1,2,0:T(8,128)(2,1)}, u32[]{:S(2)}, u32[]{:S(2)}) collective-permute-start(bf16[2,128,3,512]{3,1,2,0:T(8,128)(2,1)} %collective-permute-done.5), channel_id=1, source_target_pairs={{0,8},{8,0},{16,24},{24,16},{32,40},{40,32},{48,56},{56,48},{64,72... | collective-permute-start | bytes 2359304 | tf_op jit(solution)/shard_map/ppermute | solution.py:29
  164.8 30.5 %collective-permute-start.8 = (bf16[2,128,3,512]{3,1,2,0:T(8,128)(2,1)}, bf16[2,128,3,512]{3,1,2,0:T(8,128)(2,1)}, u32[]{:S(2)}, u32[]{:S(2)}) collective-permute-start(bf16[2,128,3,512]{3,1,2,0:T(8,128)(2,1)} %collective-permute-done.7), channel_id=1, source_target_pairs={{0,8},{8,0},{16,24},{24,16},{32,40},{40,32},{48,56},{56,48},{64,72... | collective-permute-start | bytes 2359304 | tf_op jit(solution)/shard_map/ppermute | solution.py:29
  174.2 24.6 %collective-permute-start.10 = (bf16[2,128,3,512]{3,1,2,0:T(8,128)(2,1)}, bf16[2,128,3,512]{3,1,2,0:T(8,128)(2,1)}, u32[]{:S(2)}, u32[]{:S(2)}) collective-permute-start(bf16[2,128,3,512]{3,1,2,0:T(8,128)(2,1)} %collective-permute-done.9), channel_id=1, source_target_pairs={{0,8},{8,0},{16,24},{24,16},{32,40},{40,32},{48,56},{56,48},{64,72... | collective-permute-start | bytes 2359304 | tf_op jit(solution)/shard_map/ppermute | solution.py:29
  186.4 16.0 %collective-permute-start.14 = (bf16[2,128,3,512]{3,1,2,0:T(8,128)(2,1)}, bf16[2,128,3,512]{3,1,2,0:T(8,128)(2,1)}, u32[]{:S(2)}, u32[]{:S(2)}) collective-permute-start(bf16[2,128,3,512]{3,1,2,0:T(8,128)(2,1)} %collective-permute-done.13), channel_id=1, source_target_pairs={{0,8},{8,0},{16,24},{24,16},{32,40},{40,32},{48,56},{56,48},{64,72... | collective-permute-start | bytes 2359304 | tf_op jit(solution)/shard_map/ppermute | solution.py:29
  187.8 18.1 %collective-permute-start.15 = (bf16[2,128,3,512]{3,1,2,0:T(8,128)(2,1)}, bf16[2,128,3,512]{3,1,2,0:T(8,128)(2,1)}, u32[]{:S(2)}, u32[]{:S(2)}) collective-permute-start(bf16[2,128,3,512]{3,1,2,0:T(8,128)(2,1)} %collective-permute-done.12), channel_id=1, source_target_pairs={{0,8},{8,0},{16,24},{24,16},{32,40},{40,32},{48,56},{56,48},{64,72... | collective-permute-start | bytes 2359304 | tf_op jit(solution)/shard_map/ppermute | solution.py:29
  240.7 2.3 copy-start.1
  240.7 16.4 %copy-start.4 = (bf16[512]{0:T(512)(128)(2,1)S(1)}, bf16[512]{0:T(512)(128)(2,1)}, u32[]{:S(2)}) copy-start(bf16[512]{0:T(512)(128)(2,1)} %param.17) | copy-start | bytes 3076
  244.4 2.5 collective-permute-start.17
  246.9 3.9 %collective-permute-start.18 = (f32[512]{0:T(512)S(1)}, f32[512]{0:T(512)S(1)}, u32[]{:S(2)}, u32[]{:S(2)}) collective-permute-start(f32[512]{0:T(512)S(1)} %add.153), channel_id=1, source_target_pairs={{0,2},{1,3},{2,0},{3,1},{4,6},{5,7},{6,4},{7,5},{8,10},{9,11},{10,... | collective-permute-start | bytes 6152 | tf_op jit(solution)/shard_map/ppermute | solution.py:82
  250.9 3.9 %collective-permute-start.19 = (f32[512]{0:T(512)S(1)}, f32[512]{0:T(512)S(1)}, u32[]{:S(2)}, u32[]{:S(2)}) collective-permute-start(f32[512]{0:T(512)S(1)} %add.154), channel_id=1, source_target_pairs={{0,4},{1,5},{2,6},{3,7},{4,0},{5,1},{6,2},{7,3},{8,12},{9,13},{10,... | collective-permute-start | bytes 6152 | tf_op jit(solution)/shard_map/ppermute | solution.py:82
  349.6 13.3 %slice-start = ((bf16[512,1,512]{0,2,1:T(8,128)(2,1)}), bf16[384,1,512]{0,2,1:T(8,128)(2,1)S(1)}, s32[]{:S(2)}) async-start(bf16[512,1,512]{0,2,1:T(8,128)(2,1)} %fusion.13), calls=%async_computation.4 | async-start | bytes 786432 | tf_op jit(solution)/shard_map/slice | solution.py:151
  353.2 11.8 %collective-permute-start.20 = (bf16[128,32,16]{0,2,1:T(8,128)(2,1)}, bf16[128,32,16]{0,2,1:T(8,128)(2,1)}, u32[]{:S(2)}, u32[]{:S(2)}) collective-permute-start(bf16[128,32,16]{0,2,1:T(8,128)(2,1)} %bitcast.41), channel_id=1, source_target_pairs={{0,8},{8,16},{16,24},{24,32},{32,40},{40,48},{48,56},{56,64},{64,7... | collective-permute-start | bytes 393224 | tf_op jit(solution)/shard_map/ppermute | solution.py:17
Sparse Core Ops, SparseCore 0:
  9.2 66.7 all-gather.4
  91.3 119.4 reduce-scatter.1
  257.2 80.8 all-gather.6
